TPU v7x, 256 devices: a whole 4x4x8 slice. The times are simulated.
256 devices in a mesh: dp: 8 (over x, core), expert: 32 (over y, z).
Axes of the slice: x: 4, y: 4, z: 8, core: 2. Of those that a mesh axis runs over, the one named last changes fastest.
Arguments:
- tokens: bfloat16 [32768, 2048], P(('dp', 'expert')), may hold values from -6 to 6
- router_weight: bfloat16 [2048, 64], replicated, may hold values from -0.125 to 0.125
- expert_ids: int32 [32768, 8], P(('dp', 'expert')), may hold values from 0 to 63, all different within a row; in each aligned block of 128 rows (0 to 127, 128 to 255, ...) at most 24 rows name the same one
- gate_matrix: bfloat16 [2048, 64, 384], P('dp', 'expert'), may hold values from -0.125 to 0.125
- up_matrix: bfloat16 [2048, 64, 384], P('dp', 'expert'), may hold values from -0.125 to 0.125
- down_matrix: bfloat16 [2048, 64, 384], P('dp', 'expert'), may hold values from -0.3125 to 0.3125
- cotangent: bfloat16 [32768, 2048], P(('dp', 'expert')), may hold values from -3 to 3
Outputs:
- mixed_out: bfloat16 [32768, 2048], P(('dp', 'expert'))
- token_grad: bfloat16 [32768, 2048], P(('dp', 'expert'))
- gate_grad: bfloat16 [2048, 64, 384], P('dp', 'expert')
- up_grad: bfloat16 [2048, 64, 384], P('dp', 'expert')
- down_grad: bfloat16 [2048, 64, 384], P('dp', 'expert')
- router_grad: float32 [2048, 64], replicated
Inputs may be any that keep to these rules, and one draw needn't show every extreme that they name: `expert_ids`: each row names 8 different experts and every expert is named by some row. Among the rows of one device no expert is named more than 24 times, and in some device's rows some expert is named exactly 24 times.
All inputs are finite; a program needn't handle non-finite values.
Results may differ from a plain program's by a relative error of at most 0.014.
Values may be sent and summed in bfloat16 or wider, within the bound.
No kernel may reach another device: no remote copies, remote signals or barrier semaphores. Data moves between devices by JAX's collectives and lax.ppermute only.
A program may use at most 128 MiB of HBM per device.

v0:
```python
import jax
import jax.numpy as jnp
from jax import lax
from jax.sharding import PartitionSpec as P


def shards(tokens, router_weight, expert_ids, gate_matrix, up_matrix, down_matrix, cotangent):
    highest = lax.Precision.HIGHEST
    token_count = tokens.shape[0]
    model_width = tokens.shape[1]
    top_count = expert_ids.shape[1]
    experts_total = router_weight.shape[1]
    owners = lax.axis_size("expert")
    local_experts = gate_matrix.shape[1]
    capacity = 3 * token_count * top_count // (2 * experts_total)
    logits = jnp.dot(tokens, router_weight, preferred_element_type=jnp.float32)
    expert_range = lax.iota(jnp.int32, experts_total)
    onehot = (expert_ids[:, :, None] == expert_range[None, None, :]).astype(jnp.float32)
    chosen = jnp.sum(onehot * logits[:, None, :], axis=2)
    raised = jnp.exp(chosen)
    gate_weights = raised / jnp.sum(raised, axis=1, keepdims=True)
    flat_ids = expert_ids.reshape(token_count * top_count)
    flat_hits = (flat_ids[:, None] == expert_range[None, :]).astype(jnp.int32)
    earlier = jnp.cumsum(flat_hits, axis=0) - flat_hits
    slot_index = jnp.sum(earlier * flat_hits, axis=1)
    position = flat_ids * capacity + slot_index
    picks_in = jnp.repeat(tokens, top_count, axis=0)
    send_tokens = jnp.zeros((experts_total * capacity, model_width), jnp.bfloat16)
    send_tokens = (
        send_tokens.at[position].set(picks_in).reshape(owners, local_experts, capacity, model_width)
    )
    target = cotangent.astype(jnp.float32)
    out_slope = (gate_weights[:, :, None] * target[:, None, :]).astype(jnp.bfloat16)
    send_slopes = jnp.zeros((experts_total * capacity, model_width), jnp.bfloat16)
    send_slopes = send_slopes.at[position].set(
        out_slope.reshape(token_count * top_count, model_width)
    )
    send_slopes = send_slopes.reshape(owners, local_experts, capacity, model_width)
    gate_full, up_full, down_full = (
        lax.all_gather(gate_matrix, "dp", axis=0, tiled=True),
        lax.all_gather(up_matrix, "dp", axis=0, tiled=True),
        lax.all_gather(down_matrix, "dp", axis=0, tiled=True),
    )
    received = lax.all_to_all(send_tokens, "expert", split_axis=0, concat_axis=0, tiled=True)
    pre_gate = jnp.einsum("sjcd,djf->sjcf", received, gate_full, preferred_element_type=jnp.float32)
    pre_up = jnp.einsum("sjcd,djf->sjcf", received, up_full, preferred_element_type=jnp.float32)
    expert_hidden = (jax.nn.silu(pre_gate) * pre_up).astype(jnp.bfloat16)
    outputs = jnp.einsum(
        "sjcf,djf->sjcd", expert_hidden, down_full, preferred_element_type=jnp.float32
    ).astype(jnp.bfloat16)
    pre_gate, pre_up, hidden, outputs = (pre_gate, pre_up, expert_hidden, outputs)
    returned = lax.all_to_all(outputs, "expert", split_axis=0, concat_axis=0, tiled=True)
    slopes_in = lax.all_to_all(send_slopes, "expert", split_axis=0, concat_axis=0, tiled=True)
    hidden_slope = jnp.einsum(
        "sjcd,djf->sjcf", slopes_in, down_full, preferred_element_type=jnp.float32
    )
    sigmoid_gate = jax.nn.sigmoid(pre_gate)
    activation = pre_gate * sigmoid_gate
    expert_gate_slope = (
        hidden_slope * pre_up * sigmoid_gate * (1.0 + pre_gate * (1.0 - sigmoid_gate))
    ).astype(jnp.bfloat16)
    expert_up_slope = (hidden_slope * activation).astype(jnp.bfloat16)
    pick_slope = (
        jnp.einsum(
            "sjcf,djf->sjcd", expert_gate_slope, gate_full, preferred_element_type=jnp.float32
        )
        + jnp.einsum("sjcf,djf->sjcd", expert_up_slope, up_full, preferred_element_type=jnp.float32)
    ).astype(jnp.bfloat16)
    gate_slope, up_slope, pick_slope = (expert_gate_slope, expert_up_slope, pick_slope)
    slopes_back = lax.all_to_all(pick_slope, "expert", split_axis=0, concat_axis=0, tiled=True)
    returned_rows = returned.reshape(experts_total * capacity, model_width)
    picked = jnp.take(returned_rows, position, axis=0).reshape(token_count, top_count, model_width)
    picked_f = picked.astype(jnp.float32)
    mixed_out = jnp.sum(gate_weights[:, :, None] * picked_f, axis=1).astype(jnp.bfloat16)
    gate_slope_all = jnp.sum(target[:, None, :] * picked_f, axis=2)
    centred = gate_slope_all - jnp.sum(gate_weights * gate_slope_all, axis=1, keepdims=True)
    choice_slope = gate_weights * centred
    logit_slope = jnp.sum(onehot * choice_slope[:, :, None], axis=1)
    back_rows = slopes_back.reshape(experts_total * capacity, model_width)
    input_picks = jnp.take(back_rows, position, axis=0).reshape(token_count, top_count, model_width)
    router_part = jnp.dot(logit_slope, router_weight.astype(jnp.float32).T, precision=highest)
    token_grad = (jnp.sum(input_picks.astype(jnp.float32), axis=1) + router_part).astype(
        jnp.bfloat16
    )
    router_local = jnp.dot(tokens.astype(jnp.float32).T, logit_slope, precision=highest)
    router_grad = lax.psum(router_local, ("dp", "expert"))
    grad_gate_rows = jnp.einsum(
        "sjcd,sjcf->djf", received, gate_slope, preferred_element_type=jnp.float32
    )
    grad_up_rows = jnp.einsum(
        "sjcd,sjcf->djf", received, up_slope, preferred_element_type=jnp.float32
    )
    grad_down_rows = jnp.einsum(
        "sjcd,sjcf->djf", slopes_in, hidden, preferred_element_type=jnp.float32
    )
    summed = lax.psum_scatter(
        jnp.stack([grad_gate_rows, grad_up_rows, grad_down_rows], axis=1).astype(jnp.bfloat16),
        "dp",
        scatter_dimension=0,
        tiled=True,
    )
    gate_grad = summed[:, 0]
    up_grad = summed[:, 1]
    down_grad = summed[:, 2]
    return (mixed_out, token_grad, gate_grad, up_grad, down_grad, router_grad)


def solution(mesh):
    in_specs = (
        P(("dp", "expert"), None),
        P(),
        P(("dp", "expert"), None),
        P("dp", "expert", None),
        P("dp", "expert", None),
        P("dp", "expert", None),
        P(("dp", "expert"), None),
    )
    out_specs = (
        P(("dp", "expert"), None),
        P(("dp", "expert"), None),
        P("dp", "expert", None),
        P("dp", "expert", None),
        P("dp", "expert", None),
        P(),
    )
    return jax.shard_map(shards, mesh=mesh, in_specs=in_specs, out_specs=out_specs, check_vma=False)
```

profile of v0, /device:TPU:32, one launch (start us, length us, event | category | flops | bytes accessed | tf_op | source)
XLA Modules:
  0.0 926.3 jit_solution(11587824783962643990)
XLA Ops:
  7.2 1.8 copy.77
  10.1 18.0 %reduce-window.6 = s32[64,8,128]{2,1,0:T(8,128)S(1)} reduce-window(s32[64,8,128]{2,1,0:T(8,128)S(1)} %fusion.61, s32[]{:T(128)} %constant.7.clone.1), window={size=1x1x128 pad=0_0x0_0x127_0}, to_apply=%region_2.0 | reduce-window | flops 8323072 | bytes 524292 | tf_op jit(solution)/shard_map/reduce-window
  29.6 10.2 %scatter_custom_fusion = bf16[1536,2048]{1,0:T(8,128)(2,1)} fusion(s32[1024]{0:T(1024)S(1)} %bitcast.163, bf16[]{:T(256)} %constant.15.clone.1, bf16[128,2048]{1,0:T(8,128)(2,1)S(1)} %copy-done), kind=kCustom, calls=%fused_computation.24 | custom fusion | bytes 6815746 | tf_op jit(solution)/shard_map/scatter | solution.py:30
  39.9 11.5 %all-to-all-start = ((bf16[32,2,24,2048]{3,2,1,0:T(8,128)(2,1)}), bf16[32,2,24,2048]{3,2,1,0:T(8,128)(2,1)}, u32[]{:S(2)}, u32[]{:S(2)}) async-start(bf16[32,2,24,2048]{3,2,1,0:T(8,128)(2,1)} %bitcast.158), calls=%async_computation | async-start | bytes 12582912 | tf_op jit(solution)/shard_map/all_to_all | solution.py:44
  53.4 138.8 %all-to-all-done = bf16[32,2,24,2048]{3,2,1,0:T(8,128)(2,1)} async-done(((bf16[32,2,24,2048]{3,2,1,0:T(8,128)(2,1)}), bf16[32,2,24,2048]{3,2,1,0:T(8,128)(2,1)}, u32[]{:S(2)}, u32[]{:S(2)}) %all-to-all-start) | async-done | bytes 6291488 | tf_op jit(solution)/shard_map/all_to_all | solution.py:44
  192.2 8.5 fusion.21
  200.7 9.3 %fusion.52 = (bf16[32,2,24,384]{3,2,0,1:T(8,128)(2,1)S(1)}, f32[2,32,24,384]{3,2,1,0:T(8,128)}) fusion(f32[2,32,24,384]{3,2,1,0:T(8,128)} %fusion.21, bf16[2048,2,384]{2,0,1:T(8,128)(2,1)} %all-gather.6.cloned.1.call-done, bf16[32,2,24,2048]{3,2,1,0:T(8,128)(2,1)} %all-to-all-done), kind=kOutput, calls=%fused_computation.58 | convolution fusion | flops 2419458048 | bytes 15335424 | tf_op jit(solution)/shard_map/sjcd,djf->sjcf/dot_general | solution.py:46
  210.1 6.0 convert_bitcast_fusion.1
  216.1 3.2 copy.82
  219.3 8.9 all-to-all-start.1
  229.0 139.7 %all-to-all-done.1 = bf16[32,2,24,2048]{3,2,1,0:T(8,128)(2,1)} async-done(((bf16[32,2,24,2048]{3,2,1,0:T(8,128)(2,1)}), bf16[32,2,24,2048]{3,2,1,0:T(8,128)(2,1)}, u32[]{:S(2)}, u32[]{:S(2)}) %all-to-all-start.1) | async-done | bytes 6291488 | tf_op jit(solution)/shard_map/all_to_all | solution.py:52
  368.7 12.5 %gather_fusion = bf16[1024,2048]{1,0:T(8,128)(2,1)} fusion(bf16[1536,2048]{1,0:T(8,128)(2,1)} %bitcast.15, s32[1024]{0:T(1024)S(1)} %broadcast_clamp_fusion), kind=kCustom, calls=%fused_computation.clone | custom fusion | bytes 8392704 | tf_op jit(solution)/shard_map/jit(_take)/gather | solution.py:72
  381.2 3.2 fusion.3
  384.8 10.6 %scatter_custom_fusion.1 = bf16[1536,2048]{1,0:T(8,128)(2,1)} fusion(s32[1024]{0:T(1024)S(1)} %bitcast.164, f32[128,2048]{1,0:T(8,128)S(1)} %convert_element_type.68, f32[1024]{0:T(1024)S(1)} %div.27, bf16[]{:T(256)} %constant.15.clone.1), kind=kCustom, calls=%fused_computation.23 | custom fusion | flops 4194304 | bytes 7344130 | tf_op jit(solution)/shard_map/scatter | solution.py:35
  395.4 149.1 %all_to_all.20 = bf16[32,2,24,2048]{3,2,1,0:T(8,128)(2,1)S(1)} all-to-all(bf16[32,2,24,2048]{3,2,1,0:T(8,128)(2,1)} %bitcast.159), channel_id=1, replica_groups=mesh['dp'=8,'expert'=32] {'expert'}, dimensions={0} | all-to-all | bytes 12582912 | tf_op jit(solution)/shard_map/all_to_all | solution.py:53
  544.5 3.0 fusion.44
  547.8 4.1 fusion.51
  551.9 5.4 fusion.38
  557.4 5.4 fusion.41
  562.8 4.1 pad_maximum_fusion
  567.0 8.7 fusion.31
  575.7 6.7 fusion.4
  582.4 3.8 copy.85
  586.1 6.0 all-to-all-start.3
  592.2 1.2 convolution_bitcast_fusion
  593.4 139.5 %all-to-all-done.3 = bf16[32,2,24,2048]{3,2,1,0:T(8,128)(2,1)} async-done(((bf16[32,2,24,2048]{3,2,1,0:T(8,128)(2,1)}), bf16[32,2,24,2048]{3,2,1,0:T(8,128)(2,1)}, u32[]{:S(2)}, u32[]{:S(2)}) %all-to-all-start.3) | async-done | bytes 6291488 | tf_op jit(solution)/shard_map/all_to_all | solution.py:70
  732.9 12.4 %gather_fusion.1 = bf16[1024,2048]{1,0:T(8,128)(2,1)} fusion(bf16[1536,2048]{1,0:T(8,128)(2,1)} %bitcast.24, s32[1024]{0:T(1024)S(1)} %broadcast_clamp_fusion), kind=kCustom, calls=%fused_computation.1.clone | custom fusion | bytes 8392704 | tf_op jit(solution)/shard_map/jit(_take)/gather | solution.py:80
  745.3 10.5 %convert_reduce_fusion = (f32[128,2048]{1,0:T(8,128)S(1)}, bf16[128,2048]{1,0:T(8,128)(2,1)}) fusion(bf16[1024,2048]{1,0:T(8,128)(2,1)} %gather_fusion.1, pred[1024]{0:T(1024)(128)(4,1)S(1)} %compare_and_fusion, bf16[1024,2048]{1,0:T(8,128)(2,1)} %gather_fusion, f32[128,8]{1,0:T(8,128)S(1)} %copy.71), kind=kLoop, calls=%fused_computation.13 | loop fusion | flops 14155776 | bytes 9966592 | tf_op jit(solution)/shard_map/reduce_sum | solution.py:82
  755.8 1.4 fusion.47
  757.2 1.3 slice_bitcast_fusion
  761.8 155.9 %all-reduce.2.cloned.1.call-done = f32[2048,64]{0,1:T(8,128)} async-done(((f32[2048,64]{0,1:T(8,128)}), f32[2048,64]{0,1:T(8,128)}) %all-reduce.2.cloned.1.call-update) | async-done | bytes 524304 | tf_op jit(solution)/shard_map/psum | solution.py:86
  917.7 1.9 copy.131
  (71 shorter events, 9.3 us)
Async XLA Ops:
  7.2 22.5 %copy-start = (bf16[128,2048]{1,0:T(8,128)(2,1)S(1)}, bf16[128,2048]{1,0:T(8,128)(2,1)}, u32[]{:S(2)}) copy-start(bf16[128,2048]{1,0:T(8,128)(2,1)} %param.9) | copy-start | bytes 1572868
  7.2 46.2 %all-gather.4.cloned.1.call-start = ((), (), s32[]{:S(2)}) async-start(), calls=%async_computation.5 | async-start | bytes 3538944 | tf_op jit(solution)/shard_map/all_gather | solution.py:40
  39.8 11.6 %copy-start.4 = (bf16[256,2,384]{2,1,0:T(2,128)(2,1)S(1)}, bf16[256,2,384]{2,1,0:T(2,128)(2,1)}, u32[]{:S(2)}) copy-start(bf16[256,2,384]{2,1,0:T(2,128)(2,1)} %param.13) | copy-start | bytes 1179652
  39.9 12.7 %copy-start.5 = (bf16[256,2,384]{2,1,0:T(2,128)(2,1)S(1)}, bf16[256,2,384]{2,1,0:T(2,128)(2,1)}, u32[]{:S(2)}) copy-start(bf16[256,2,384]{2,1,0:T(2,128)(2,1)} %param.14) | copy-start | bytes 1179652
  39.9 152.4 %all-to-all-start = ((bf16[32,2,24,2048]{3,2,1,0:T(8,128)(2,1)}), bf16[32,2,24,2048]{3,2,1,0:T(8,128)(2,1)}, u32[]{:S(2)}, u32[]{:S(2)}) async-start(bf16[32,2,24,2048]{3,2,1,0:T(8,128)(2,1)} %bitcast.158), calls=%async_computation | async-start | bytes 12582912 | tf_op jit(solution)/shard_map/all_to_all | solution.py:44
  51.4 149.3 %all-gather.6.cloned.1.call-start = ((), (), s32[]{:S(2)}) async-start(), calls=%async_computation.6 | async-start | bytes 3538944 | tf_op jit(solution)/shard_map/all_gather | solution.py:41
  52.3 157.8 %all-gather.8.cloned.1.call-start = ((), (), s32[]{:S(2)}) async-start(), calls=%async_computation.7 | async-start | bytes 3538944 | tf_op jit(solution)/shard_map/all_gather | solution.py:42
  210.1 6.0 copy-start.8
  219.3 9.2 copy-start.3
  219.3 9.3 %copy-start.2 = (bf16[2048,64]{0,1:T(8,128)(2,1)S(1)}, bf16[2048,64]{0,1:T(8,128)(2,1)}, u32[]{:S(2)}) copy-start(bf16[2048,64]{0,1:T(8,128)(2,1)} %param.10) | copy-start | bytes 786436
  219.3 9.6 %copy-start.6 = (s32[128,8]{0,1:T(8,128)S(1)}, s32[128,8]{0,1:T(8,128)}, u32[]{:S(2)}) copy-start(s32[128,8]{0,1:T(8,128)} %param.11) | copy-start | bytes 12292
  219.3 149.4 %all-to-all-start.1 = ((bf16[32,2,24,2048]{3,2,1,0:T(8,128)(2,1)}), bf16[32,2,24,2048]{3,2,1,0:T(8,128)(2,1)}, u32[]{:S(2)}, u32[]{:S(2)}) async-start(bf16[32,2,24,2048]{3,2,1,0:T(8,128)(2,1)} %copy.82), calls=%async_computation.1 | async-start | bytes 12582912 | tf_op jit(solution)/shard_map/all_to_all | solution.py:52
  228.2 529.0 %reduce-scatter.2.cloned.1.call-start = ((), (), s32[]{:S(2)}) async-start(), calls=%async_computation.8 | async-start | bytes 10616832 | tf_op jit(solution)/shard_map/reduce_scatter | solution.py:96
  395.4 149.1 %copy-start.9 = (bf16[32,2,24,384]{3,2,0,1:T(8,128)(2,1)S(1)}, bf16[32,2,24,384]{3,2,0,1:T(8,128)(2,1)}, u32[]{:S(2)}) copy-start(bf16[32,2,24,384]{3,2,0,1:T(8,128)(2,1)} %copy-done.8) | copy-start | bytes 3538948
  544.5 3.0 copy-start.7
  544.5 3.0 copy-start.10
  544.5 3.3 copy-start.11
  567.0 8.7 copy-start.1
  586.1 146.7 %all-to-all-start.3 = ((bf16[32,2,24,2048]{3,2,1,0:T(8,128)(2,1)}), bf16[32,2,24,2048]{3,2,1,0:T(8,128)(2,1)}, u32[]{:S(2)}, u32[]{:S(2)}) async-start(bf16[32,2,24,2048]{3,2,1,0:T(8,128)(2,1)} %copy.85), calls=%async_computation.3 | async-start | bytes 12582912 | tf_op jit(solution)/shard_map/all_to_all | solution.py:70
  592.1 325.6 %all-reduce.2.cloned.1.call-start = ((), (), s32[]{:S(2)}) async-start(), calls=%async_computation.9 | async-start | bytes 1048576 | tf_op jit(solution)/shard_map/psum | solution.py:86
Sparse Core Ops, SparseCore 0:
  10.4 32.8 all-gather.3
  54.6 31.2 all-gather.5
  88.3 30.1 all-gather.7
  567.1 56.4 reduce-scatter.1
  629.4 288.2 all-reduce.1
where the time goes:
time: 935 us; the launch traced here: 926 us
  waiting for transfers between devices  574 us (61%)
  blocking collectives  149 us (16%)
  matrix products  60.1 us (6%)
  local copies, waits for them, and re-layouts  54.1 us (6%)
  other arithmetic  47.7 us (5%)
  starting transfers between devices  27 us (3%)
  between operations  14.3 us (2%)
    psum x1, waiting for transfers between devices, shards(): router_grad = lax.psum(router_local, ('dp', 'expert'))  156 us
    all_to_all x1, blocking collectives, shards(): lax.all_to_all(send_slopes, 'expert', split_axis=0, concat_axis=0, tiled=...  149 us
    all_to_all x1, waiting for transfers between devices, shards(): lax.all_to_all(outputs, 'expert', split_axis=0, concat_axis=0, tiled=True)  140 us
    all_to_all x1, waiting for transfers between devices, shards(): lax.all_to_all(pick_slope, 'expert', split_axis=0, concat_axis=0, tiled=T...  140 us
    all_to_all x1, waiting for transfers between devices, shards(): lax.all_to_all(send_tokens, 'expert', split_axis=0, concat_axis=0, tiled=...  139 us
  transfers between devices with their start and end apart: 8, of which 4 were waited for; matrix products, arithmetic and copies ran while one was open for 11% of the time, Pallas kernels for 0%

commit v1 on v0

--- a/solution.py
+++ b/solution.py
@@ -13,29 +13,38 @@
     owners = lax.axis_size("expert")
     local_experts = gate_matrix.shape[1]
     capacity = 3 * token_count * top_count // (2 * experts_total)
+    pick_count = token_count * top_count
+    slot_count = experts_total * capacity
     logits = jnp.dot(tokens, router_weight, preferred_element_type=jnp.float32)
     expert_range = lax.iota(jnp.int32, experts_total)
     onehot = (expert_ids[:, :, None] == expert_range[None, None, :]).astype(jnp.float32)
     chosen = jnp.sum(onehot * logits[:, None, :], axis=2)
     raised = jnp.exp(chosen)
     gate_weights = raised / jnp.sum(raised, axis=1, keepdims=True)
-    flat_ids = expert_ids.reshape(token_count * top_count)
-    flat_hits = (flat_ids[:, None] == expert_range[None, :]).astype(jnp.int32)
-    earlier = jnp.cumsum(flat_hits, axis=0) - flat_hits
-    slot_index = jnp.sum(earlier * flat_hits, axis=1)
-    position = flat_ids * capacity + slot_index
-    picks_in = jnp.repeat(tokens, top_count, axis=0)
-    send_tokens = jnp.zeros((experts_total * capacity, model_width), jnp.bfloat16)
+    flat_ids = expert_ids.reshape(pick_count)
+    flat_hits = (flat_ids[:, None] == expert_range[None, :]).astype(jnp.bfloat16)
+    pick_range = lax.iota(jnp.int32, pick_count)
+    before = (pick_range[None, :] < pick_range[:, None]).astype(jnp.bfloat16)
+    earlier = jnp.dot(before, flat_hits, preferred_element_type=jnp.float32)
+    slot_index = jnp.sum(earlier * flat_hits.astype(jnp.float32), axis=1).astype(jnp.int32)
+    position = (flat_ids * capacity + slot_index).reshape(token_count, top_count)
+    slot_range = lax.iota(jnp.int32, slot_count)
+    slot_hits = position[None, :, :] == slot_range[:, None, None]
+    slot_token = jnp.any(slot_hits, axis=2)
+    slot_token_b = slot_token.astype(jnp.bfloat16)
+    slot_gate = jnp.sum(jnp.where(slot_hits, gate_weights[None, :, :], 0.0), axis=(1, 2))
     send_tokens = (
-        send_tokens.at[position].set(picks_in).reshape(owners, local_experts, capacity, model_width)
+        jnp.dot(slot_token_b, tokens, preferred_element_type=jnp.float32)
+        .astype(jnp.bfloat16)
+        .reshape(owners, local_experts, capacity, model_width)
     )
     target = cotangent.astype(jnp.float32)
-    out_slope = (gate_weights[:, :, None] * target[:, None, :]).astype(jnp.bfloat16)
-    send_slopes = jnp.zeros((experts_total * capacity, model_width), jnp.bfloat16)
-    send_slopes = send_slopes.at[position].set(
-        out_slope.reshape(token_count * top_count, model_width)
+    slot_target = jnp.dot(slot_token_b, cotangent, preferred_element_type=jnp.float32)
+    send_slopes = (
+        (slot_gate[:, None] * slot_target)
+        .astype(jnp.bfloat16)
+        .reshape(owners, local_experts, capacity, model_width)
     )
-    send_slopes = send_slopes.reshape(owners, local_experts, capacity, model_width)
     gate_full, up_full, down_full = (
         lax.all_gather(gate_matrix, "dp", axis=0, tiled=True),
         lax.all_gather(up_matrix, "dp", axis=0, tiled=True),
@@ -48,8 +57,32 @@
     outputs = jnp.einsum(
         "sjcf,djf->sjcd", expert_hidden, down_full, preferred_element_type=jnp.float32
     ).astype(jnp.bfloat16)
-    pre_gate, pre_up, hidden, outputs = (pre_gate, pre_up, expert_hidden, outputs)
+    hidden = expert_hidden
     returned = lax.all_to_all(outputs, "expert", split_axis=0, concat_axis=0, tiled=True)
+    returned_rows = returned.reshape(slot_count, model_width)
+    slot_mix = jnp.where(slot_token.T, slot_gate[None, :], 0.0)
+    mix_high = slot_mix.astype(jnp.bfloat16)
+    mix_low = (slot_mix - mix_high.astype(jnp.float32)).astype(jnp.bfloat16)
+    mixed_out = (
+        jnp.dot(mix_high, returned_rows, preferred_element_type=jnp.float32)
+        + jnp.dot(mix_low, returned_rows, preferred_element_type=jnp.float32)
+    ).astype(jnp.bfloat16)
+    token_slot_slope = lax.dot_general(
+        cotangent, returned_rows, (((1,), (1,)), ((), ())), preferred_element_type=jnp.float32
+    )
+    gate_slope_all = jnp.take_along_axis(token_slot_slope, position, axis=1)
+    centred = gate_slope_all - jnp.sum(gate_weights * gate_slope_all, axis=1, keepdims=True)
+    choice_slope = gate_weights * centred
+    logit_slope = jnp.sum(onehot * choice_slope[:, :, None], axis=1)
+    router_local = jnp.dot(tokens.astype(jnp.float32).T, logit_slope, precision=highest)
+    send_slopes, router_local = lax.optimization_barrier((send_slopes, router_local))
+    row_parts = router_local.reshape(owners, model_width // owners, experts_total)
+    row_parts = lax.all_to_all(row_parts, "expert", split_axis=0, concat_axis=0, tiled=True)
+    row_block = lax.psum(jnp.sum(row_parts, axis=0), "dp")
+    row_copies = jnp.broadcast_to(row_block[None], (owners,) + row_block.shape)
+    router_grad = lax.all_to_all(
+        row_copies, "expert", split_axis=0, concat_axis=0, tiled=True
+    ).reshape(model_width, experts_total)
     slopes_in = lax.all_to_all(send_slopes, "expert", split_axis=0, concat_axis=0, tiled=True)
     hidden_slope = jnp.einsum(
         "sjcd,djf->sjcf", slopes_in, down_full, preferred_element_type=jnp.float32
@@ -66,24 +99,14 @@
         )
         + jnp.einsum("sjcf,djf->sjcd", expert_up_slope, up_full, preferred_element_type=jnp.float32)
     ).astype(jnp.bfloat16)
-    gate_slope, up_slope, pick_slope = (expert_gate_slope, expert_up_slope, pick_slope)
+    gate_slope, up_slope = (expert_gate_slope, expert_up_slope)
     slopes_back = lax.all_to_all(pick_slope, "expert", split_axis=0, concat_axis=0, tiled=True)
-    returned_rows = returned.reshape(experts_total * capacity, model_width)
-    picked = jnp.take(returned_rows, position, axis=0).reshape(token_count, top_count, model_width)
-    picked_f = picked.astype(jnp.float32)
-    mixed_out = jnp.sum(gate_weights[:, :, None] * picked_f, axis=1).astype(jnp.bfloat16)
-    gate_slope_all = jnp.sum(target[:, None, :] * picked_f, axis=2)
-    centred = gate_slope_all - jnp.sum(gate_weights * gate_slope_all, axis=1, keepdims=True)
-    choice_slope = gate_weights * centred
-    logit_slope = jnp.sum(onehot * choice_slope[:, :, None], axis=1)
-    back_rows = slopes_back.reshape(experts_total * capacity, model_width)
-    input_picks = jnp.take(back_rows, position, axis=0).reshape(token_count, top_count, model_width)
+    back_rows = slopes_back.reshape(slot_count, model_width)
+    input_sum = lax.dot_general(
+        slot_token_b, back_rows, (((0,), (0,)), ((), ())), preferred_element_type=jnp.float32
+    )
     router_part = jnp.dot(logit_slope, router_weight.astype(jnp.float32).T, precision=highest)
-    token_grad = (jnp.sum(input_picks.astype(jnp.float32), axis=1) + router_part).astype(
-        jnp.bfloat16
-    )
-    router_local = jnp.dot(tokens.astype(jnp.float32).T, logit_slope, precision=highest)
-    router_grad = lax.psum(router_local, ("dp", "expert"))
+    token_grad = (input_sum + router_part).astype(jnp.bfloat16)
     grad_gate_rows = jnp.einsum(
         "sjcd,sjcf->djf", received, gate_slope, preferred_element_type=jnp.float32
     )

time: 935 us -> 799 us (0.85)
  waiting for transfers between devices: 574 us -> 400 us
  blocking collectives: 149 us -> 195 us
  matrix products: 60.1 us -> 84.5 us
  local copies, waits for them, and re-layouts: 54.1 us -> 32.5 us
  other arithmetic: 47.7 us -> 26.3 us
  starting transfers between devices: 27 us -> 37 us
    psum x1 -> x0, waiting for transfers between devices: 156 us -> none  [shards(): router_grad = lax.psum(router_local, ('dp', 'expert'))]
    psum x0 -> x1, blocking collectives: none -> 24.5 us  [shards(): row_block = lax.psum(jnp.sum(row_parts, axis=0), 'dp')]
    dot_general x0 -> x7, matrix products: none -> 23.9 us  [the longest x1 4.68 us: shards(): jnp.dot(mix_low, returned_rows, preferred_element_type=jnp.float32)]
    all_to_all x0 -> x1, blocking collectives: none -> 22.3 us  [shards(): lax.all_to_all(row_parts, 'expert', split_axis=0, concat_axis=0, tiled=True)]
    another operation x3 -> x0, other arithmetic: 18.2 us -> none
    all_to_all x1, waiting for transfers between devices: 140 us -> 122 us  [shards(): lax.all_to_all(pick_slope, 'expert', split_axis=0, concat_axis=0, tiled=T...]
    gather x2 -> x5, local copies, waits for them, and re-layouts: 24.9 us -> 7.34 us  [shards(): gate_slope_all = jnp.take_along_axis(token_slot_slope, position, axis=1)]
    scatter x1 -> x0, other arithmetic: 10.6 us -> none  [shards(): send_slopes.at[position]]
  transfers between devices with their start and end apart: 8 -> 8, of which waited for: 4 -> 4; matrix products, arithmetic and copies ran while one was open for 11% -> 10% of each run, Pallas kernels for 0% -> 0%
where the time goes in v1:
time: 799 us; the launch traced here: 790 us
  waiting for transfers between devices  400 us (50%)
  blocking collectives  195 us (24%)
  matrix products  84.5 us (11%)
  starting transfers between devices  37 us (5%)
  local copies, waits for them, and re-layouts  32.5 us (4%)
  other arithmetic  26.3 us (3%)
  between operations  14.4 us (2%)
    all_to_all x1, blocking collectives, shards(): lax.all_to_all(send_slopes, 'expert', split_axis=0, concat_axis=0, tiled=...  149 us
    all_to_all x1, waiting for transfers between devices, shards(): lax.all_to_all(outputs, 'expert', split_axis=0, concat_axis=0, tiled=True)  139 us
    all_to_all x1, waiting for transfers between devices, shards(): lax.all_to_all(send_tokens, 'expert', split_axis=0, concat_axis=0, tiled=...  130 us
    all_to_all x1, waiting for transfers between devices, shards(): lax.all_to_all(pick_slope, 'expert', split_axis=0, concat_axis=0, tiled=T...  122 us
    psum x1, blocking collectives, shards(): row_block = lax.psum(jnp.sum(row_parts, axis=0), 'dp')  24.5 us
    all_to_all x1, blocking collectives, shards(): lax.all_to_all(row_parts, 'expert', split_axis=0, concat_axis=0, tiled=True)  22.3 us
  transfers between devices with their start and end apart: 8, of which 4 were waited for; matrix products, arithmetic and copies ran while one was open for 10% of the time, Pallas kernels for 0%

profile of v1, /device:TPU:32, one launch (start us, length us, event | category | flops | bytes accessed | tf_op | source)
XLA Modules:
  0.0 790.2 jit_solution(6979990240944075010)
XLA Ops:
  10.8 5.6 fusion.1
  16.4 4.4 convolution_convert_fusion
  20.8 11.5 %all-to-all-start = ((bf16[32,2,24,2048]{3,2,1,0:T(8,128)(2,1)}), bf16[32,2,24,2048]{3,2,1,0:T(8,128)(2,1)}, u32[]{:S(2)}, u32[]{:S(2)}) async-start(bf16[32,2,24,2048]{3,2,1,0:T(8,128)(2,1)} %bitcast.156), calls=%async_computation | async-start | bytes 12582912 | tf_op jit(solution)/shard_map/all_to_all | solution.py:53
  34.4 8.9 %all-gather.4.cloned.1.call-done = bf16[2048,2,384]{2,0,1:T(8,128)(2,1)} async-done(((bf16[256,2,384]{2,0,1:T(8,128)(2,1)}), bf16[2048,2,384]{2,0,1:T(8,128)(2,1)}) %all-gather.4.cloned.1.call-update) | async-done | bytes 3145744 | tf_op jit(solution)/shard_map/all_gather | solution.py:49
  43.3 129.9 %all-to-all-done = bf16[32,2,24,2048]{3,2,1,0:T(8,128)(2,1)} async-done(((bf16[32,2,24,2048]{3,2,1,0:T(8,128)(2,1)}), bf16[32,2,24,2048]{3,2,1,0:T(8,128)(2,1)}, u32[]{:S(2)}, u32[]{:S(2)}) %all-to-all-start) | async-done | bytes 6291488 | tf_op jit(solution)/shard_map/all_to_all | solution.py:53
  173.2 8.6 %fusion.13 = f32[2,32,24,384]{3,2,1,0:T(8,128)} fusion(bf16[32,2,24,2048]{3,2,1,0:T(8,128)(2,1)} %all-to-all-done, bf16[2048,2,384]{2,0,1:T(8,128)(2,1)} %all-gather.4.cloned.1.call-done), kind=kOutput, calls=%fused_computation.25 | convolution fusion | flops 2415919104 | bytes 11796480 | tf_op jit(solution)/shard_map/sjcd,djf->sjcf/dot_general | solution.py:54
  181.8 9.4 %fusion.43 = (bf16[32,2,24,384]{3,2,0,1:T(8,128)(2,1)S(1)}, f32[2,32,24,384]{3,2,1,0:T(8,128)}) fusion(f32[2,32,24,384]{3,2,1,0:T(8,128)} %fusion.13, bf16[2048,2,384]{2,0,1:T(8,128)(2,1)} %all-gather.6.cloned.1.call-done, bf16[32,2,24,2048]{3,2,1,0:T(8,128)(2,1)} %all-to-all-done), kind=kOutput, calls=%fused_computation.49 | convolution fusion | flops 2419458048 | bytes 15335424 | tf_op jit(solution)/shard_map/sjcd,djf->sjcf/dot_general | solution.py:55
  191.2 6.0 convert_bitcast_fusion
  197.2 3.2 copy.101
  200.4 8.9 %all-to-all-start.1 = ((bf16[32,2,24,2048]{3,2,1,0:T(8,128)(2,1)}), bf16[32,2,24,2048]{3,2,1,0:T(8,128)(2,1)}, u32[]{:S(2)}, u32[]{:S(2)}) async-start(bf16[32,2,24,2048]{3,2,1,0:T(8,128)(2,1)} %copy.101), calls=%async_computation.1 | async-start | bytes 12582912 | tf_op jit(solution)/shard_map/all_to_all | solution.py:61
  210.4 139.3 %all-to-all-done.1 = bf16[32,2,24,2048]{3,2,1,0:T(8,128)(2,1)} async-done(((bf16[32,2,24,2048]{3,2,1,0:T(8,128)(2,1)}), bf16[32,2,24,2048]{3,2,1,0:T(8,128)(2,1)}, u32[]{:S(2)}, u32[]{:S(2)}) %all-to-all-start.1) | async-done | bytes 6291488 | tf_op jit(solution)/shard_map/all_to_all | solution.py:61
  349.8 4.6 convolution_bitcast_fusion
  354.4 7.0 gather_fusion
  361.6 11.5 %select_reduce_fusion = f32[1536]{0:T(1024)S(1)} fusion(f32[128,8]{0,1:T(8,128)S(1)} %get-tuple-element.41, s32[128,8]{0,1:T(8,128)S(1)} %get-tuple-element.43), kind=kLoop, calls=%fused_computation.10 | loop fusion | flops 4717056 | bytes 14336 | tf_op jit(solution)/shard_map/reduce_sum | solution.py:35
  375.3 148.7 %all_to_all.30 = bf16[32,2,24,2048]{3,2,1,0:T(8,128)(2,1)S(1)} all-to-all(bf16[32,2,24,2048]{3,2,1,0:T(8,128)(2,1)S(1)} %bitcast.155), channel_id=1, replica_groups=mesh['dp'=8,'expert'=32] {'expert'}, dimensions={0} | all-to-all | bytes 12582912 | tf_op jit(solution)/shard_map/all_to_all | solution.py:86
  524.0 3.0 fusion.34
  527.0 5.6 fusion.42
  532.6 6.3 fusion.31
  538.9 5.5 fusion.28
  544.4 4.1 pad_maximum_fusion
  550.2 22.3 %all_to_all.31 = f32[32,1,4096]{2,1,0:T(1,128)S(1)} all-to-all(f32[32,1,4096]{2,1,0:T(1,128)S(1)} %reshape.115), channel_id=1, replica_groups=mesh['dp'=8,'expert'=32] {'expert'}, dimensions={0} | all-to-all | bytes 1048576 | tf_op jit(solution)/shard_map/all_to_all | solution.py:80
  575.5 24.5 %psum.7 = f32[64,64]{0,1:T(8,128)S(1)} all-reduce(f32[64,64]{0,1:T(8,128)S(1)} %bitcast_reduce_fusion), channel_id=1, replica_groups=mesh['dp'=8,'expert'=32] {'dp'}, use_global_device_ids=true, to_apply=%region_9.10 | all-reduce | flops 4096 | bytes 32768 | tf_op jit(solution)/shard_map/psum | solution.py:81
  601.5 5.4 all-to-all-start.5
  606.9 5.7 fusion.23
  612.6 8.4 %fusion = bf16[32,2,24,2048]{3,2,0,1:T(8,128)(2,1)} fusion(f32[2,32,24,2048]{3,2,1,0:T(8,128)S(1)} %fusion.23, bf16[32,2,24,384]{3,2,0,1:T(8,128)(2,1)} %copy-done.3, bf16[2048,2,384]{2,0,1:T(8,128)(2,1)} %all-gather.6.cloned.1.call-done), kind=kOutput, calls=%fused_computation.5 | convolution fusion | flops 2422210560 | bytes 23199744 | tf_op jit(solution)/shard_map/sjcf,djf->sjcd/dot_general | solution.py:100
  621.0 6.5 copy.105
  627.6 10.3 %all-to-all-start.3 = ((bf16[32,2,24,2048]{3,2,1,0:T(8,128)(2,1)}), bf16[32,2,24,2048]{3,2,1,0:T(8,128)(2,1)}, u32[]{:S(2)}, u32[]{:S(2)}) async-start(bf16[32,2,24,2048]{3,2,1,0:T(8,128)(2,1)} %copy.105), calls=%async_computation.3 | async-start | bytes 12582912 | tf_op jit(solution)/shard_map/all_to_all | solution.py:103
  637.8 3.9 fusion.51
  641.7 4.7 fusion.37
  646.4 2.9 reduce.1
  651.5 121.8 %all-to-all-done.3 = bf16[32,2,24,2048]{3,2,1,0:T(8,128)(2,1)} async-done(((bf16[32,2,24,2048]{3,2,1,0:T(8,128)(2,1)}), bf16[32,2,24,2048]{3,2,1,0:T(8,128)(2,1)}, u32[]{:S(2)}, u32[]{:S(2)}) %all-to-all-start.3) | async-done | bytes 6291488 | tf_op jit(solution)/shard_map/all_to_all | solution.py:103
  773.4 3.9 fusion.62
  (79 shorter events, 23.4 us)
Async XLA Ops:
  7.2 342.6 %copy-start = (bf16[128,2048]{1,0:T(8,128)(2,1)S(1)}, bf16[128,2048]{1,0:T(8,128)(2,1)}, u32[]{:S(2)}) copy-start(bf16[128,2048]{1,0:T(8,128)(2,1)} %param.13) | copy-start | bytes 1572868
  7.2 3.6 copy-start.9
  7.2 9.2 %copy-start.2 = (bf16[128,2048]{1,0:T(8,128)(2,1)S(1)}, bf16[128,2048]{1,0:T(8,128)(2,1)}, u32[]{:S(2)}) copy-start(bf16[128,2048]{1,0:T(8,128)(2,1)} %param.7) | copy-start | bytes 1572868
  7.2 36.1 %all-gather.4.cloned.1.call-start = ((), (), s32[]{:S(2)}) async-start(), calls=%async_computation.7 | async-start | bytes 3538944 | tf_op jit(solution)/shard_map/all_gather | solution.py:49
  20.8 11.6 %copy-start.7 = (bf16[256,2,384]{2,1,0:T(2,128)(2,1)S(1)}, bf16[256,2,384]{2,1,0:T(2,128)(2,1)}, u32[]{:S(2)}) copy-start(bf16[256,2,384]{2,1,0:T(2,128)(2,1)} %param.11) | copy-start | bytes 1179652
  20.8 12.8 %copy-start.8 = (bf16[256,2,384]{2,1,0:T(2,128)(2,1)S(1)}, bf16[256,2,384]{2,1,0:T(2,128)(2,1)}, u32[]{:S(2)}) copy-start(bf16[256,2,384]{2,1,0:T(2,128)(2,1)} %param.12) | copy-start | bytes 1179652
  20.8 152.3 %all-to-all-start = ((bf16[32,2,24,2048]{3,2,1,0:T(8,128)(2,1)}), bf16[32,2,24,2048]{3,2,1,0:T(8,128)(2,1)}, u32[]{:S(2)}, u32[]{:S(2)}) async-start(bf16[32,2,24,2048]{3,2,1,0:T(8,128)(2,1)} %bitcast.156), calls=%async_computation | async-start | bytes 12582912 | tf_op jit(solution)/shard_map/all_to_all | solution.py:53
  32.4 149.4 %all-gather.6.cloned.1.call-start = ((), (), s32[]{:S(2)}) async-start(), calls=%async_computation.8 | async-start | bytes 3538944 | tf_op jit(solution)/shard_map/all_gather | solution.py:50
  33.3 157.9 %all-gather.8.cloned.1.call-start = ((), (), s32[]{:S(2)}) async-start(), calls=%async_computation.9 | async-start | bytes 3538944 | tf_op jit(solution)/shard_map/all_gather | solution.py:51
  191.2 6.0 copy-start.11
  200.4 9.7 %copy-start.5 = (bf16[2048,64]{0,1:T(8,128)(2,1)S(1)}, bf16[2048,64]{0,1:T(8,128)(2,1)}, u32[]{:S(2)}) copy-start(bf16[2048,64]{0,1:T(8,128)(2,1)} %param.8) | copy-start | bytes 786436
  200.4 149.3 %all-to-all-start.1 = ((bf16[32,2,24,2048]{3,2,1,0:T(8,128)(2,1)}), bf16[32,2,24,2048]{3,2,1,0:T(8,128)(2,1)}, u32[]{:S(2)}, u32[]{:S(2)}) async-start(bf16[32,2,24,2048]{3,2,1,0:T(8,128)(2,1)} %copy.101), calls=%async_computation.1 | async-start | bytes 12582912 | tf_op jit(solution)/shard_map/all_to_all | solution.py:61
  209.3 569.5 %reduce-scatter.2.cloned.1.call-start = ((), (), s32[]{:S(2)}) async-start(), calls=%async_computation.10 | async-start | bytes 10616832 | tf_op jit(solution)/shard_map/reduce_scatter | solution.py:119
  375.2 148.7 %copy-start.12 = (bf16[32,2,24,384]{3,2,0,1:T(8,128)(2,1)S(1)}, bf16[32,2,24,384]{3,2,0,1:T(8,128)(2,1)}, u32[]{:S(2)}) copy-start(bf16[32,2,24,384]{3,2,0,1:T(8,128)(2,1)} %copy-done.11) | copy-start | bytes 3538948
  524.0 3.0 copy-start.10
  524.0 3.0 copy-start.13
  532.5 6.4 copy-start.3
  532.6 6.4 copy-start.4
  601.5 26.1 %all-to-all-start.5 = ((f32[32,1,4096]{2,1,0:T(1,128)}), f32[32,1,4096]{2,1,0:T(1,128)}, u32[]{:S(2)}, u32[]{:S(2)}) async-start(f32[32,1,4096]{2,1,0:T(1,128)} %reshape.117), calls=%async_computation.6 | async-start | bytes 1048576 | tf_op jit(solution)/shard_map/all_to_all | solution.py:83
  627.6 145.8 %all-to-all-start.3 = ((bf16[32,2,24,2048]{3,2,1,0:T(8,128)(2,1)}), bf16[32,2,24,2048]{3,2,1,0:T(8,128)(2,1)}, u32[]{:S(2)}, u32[]{:S(2)}) async-start(bf16[32,2,24,2048]{3,2,1,0:T(8,128)(2,1)} %copy.105), calls=%async_computation.3 | async-start | bytes 12582912 | tf_op jit(solution)/shard_map/all_to_all | solution.py:103
  773.4 3.9 copy-start.6
  773.4 10.0 %copy-start.1 = (bf16[128,2048]{1,0:T(8,128)(2,1)S(1)}, bf16[128,2048]{1,0:T(8,128)(2,1)}, u32[]{:S(2)}) copy-start(bf16[128,2048]{1,0:T(8,128)(2,1)} %param.13) | copy-start | bytes 1572868
Sparse Core Ops, SparseCore 0:
  10.4 32.8 all-gather.3
  45.7 30.1 all-gather.5
  78.3 30.1 all-gather.7
  548.7 56.7 reduce-scatter.1

commit v2 on v1

--- a/solution.py
+++ b/solution.py
@@ -38,7 +38,6 @@
         .astype(jnp.bfloat16)
         .reshape(owners, local_experts, capacity, model_width)
     )
-    target = cotangent.astype(jnp.float32)
     slot_target = jnp.dot(slot_token_b, cotangent, preferred_element_type=jnp.float32)
     send_slopes = (
         (slot_gate[:, None] * slot_target)
@@ -50,7 +49,15 @@
         lax.all_gather(up_matrix, "dp", axis=0, tiled=True),
         lax.all_gather(down_matrix, "dp", axis=0, tiled=True),
     )
-    received = lax.all_to_all(send_tokens, "expert", split_axis=0, concat_axis=0, tiled=True)
+    dispatched = lax.all_to_all(
+        jnp.concatenate([send_tokens, send_slopes], axis=3),
+        "expert",
+        split_axis=0,
+        concat_axis=0,
+        tiled=True,
+    )
+    received = dispatched[..., :model_width]
+    slopes_in = dispatched[..., model_width:]
     pre_gate = jnp.einsum("sjcd,djf->sjcf", received, gate_full, preferred_element_type=jnp.float32)
     pre_up = jnp.einsum("sjcd,djf->sjcf", received, up_full, preferred_element_type=jnp.float32)
     expert_hidden = (jax.nn.silu(pre_gate) * pre_up).astype(jnp.bfloat16)
@@ -58,32 +65,6 @@
         "sjcf,djf->sjcd", expert_hidden, down_full, preferred_element_type=jnp.float32
     ).astype(jnp.bfloat16)
     hidden = expert_hidden
-    returned = lax.all_to_all(outputs, "expert", split_axis=0, concat_axis=0, tiled=True)
-    returned_rows = returned.reshape(slot_count, model_width)
-    slot_mix = jnp.where(slot_token.T, slot_gate[None, :], 0.0)
-    mix_high = slot_mix.astype(jnp.bfloat16)
-    mix_low = (slot_mix - mix_high.astype(jnp.float32)).astype(jnp.bfloat16)
-    mixed_out = (
-        jnp.dot(mix_high, returned_rows, preferred_element_type=jnp.float32)
-        + jnp.dot(mix_low, returned_rows, preferred_element_type=jnp.float32)
-    ).astype(jnp.bfloat16)
-    token_slot_slope = lax.dot_general(
-        cotangent, returned_rows, (((1,), (1,)), ((), ())), preferred_element_type=jnp.float32
-    )
-    gate_slope_all = jnp.take_along_axis(token_slot_slope, position, axis=1)
-    centred = gate_slope_all - jnp.sum(gate_weights * gate_slope_all, axis=1, keepdims=True)
-    choice_slope = gate_weights * centred
-    logit_slope = jnp.sum(onehot * choice_slope[:, :, None], axis=1)
-    router_local = jnp.dot(tokens.astype(jnp.float32).T, logit_slope, precision=highest)
-    send_slopes, router_local = lax.optimization_barrier((send_slopes, router_local))
-    row_parts = router_local.reshape(owners, model_width // owners, experts_total)
-    row_parts = lax.all_to_all(row_parts, "expert", split_axis=0, concat_axis=0, tiled=True)
-    row_block = lax.psum(jnp.sum(row_parts, axis=0), "dp")
-    row_copies = jnp.broadcast_to(row_block[None], (owners,) + row_block.shape)
-    router_grad = lax.all_to_all(
-        row_copies, "expert", split_axis=0, concat_axis=0, tiled=True
-    ).reshape(model_width, experts_total)
-    slopes_in = lax.all_to_all(send_slopes, "expert", split_axis=0, concat_axis=0, tiled=True)
     hidden_slope = jnp.einsum(
         "sjcd,djf->sjcf", slopes_in, down_full, preferred_element_type=jnp.float32
     )
@@ -100,8 +81,37 @@
         + jnp.einsum("sjcf,djf->sjcd", expert_up_slope, up_full, preferred_element_type=jnp.float32)
     ).astype(jnp.bfloat16)
     gate_slope, up_slope = (expert_gate_slope, expert_up_slope)
-    slopes_back = lax.all_to_all(pick_slope, "expert", split_axis=0, concat_axis=0, tiled=True)
-    back_rows = slopes_back.reshape(slot_count, model_width)
+    gathered = lax.all_to_all(
+        jnp.concatenate([outputs, pick_slope], axis=3),
+        "expert",
+        split_axis=0,
+        concat_axis=0,
+        tiled=True,
+    )
+    returned_rows = gathered[..., :model_width].reshape(slot_count, model_width)
+    back_rows = gathered[..., model_width:].reshape(slot_count, model_width)
+    slot_mix = jnp.where(slot_token.T, slot_gate[None, :], 0.0)
+    mix_high = slot_mix.astype(jnp.bfloat16)
+    mix_low = (slot_mix - mix_high.astype(jnp.float32)).astype(jnp.bfloat16)
+    mixed_out = (
+        jnp.dot(mix_high, returned_rows, preferred_element_type=jnp.float32)
+        + jnp.dot(mix_low, returned_rows, preferred_element_type=jnp.float32)
+    ).astype(jnp.bfloat16)
+    token_slot_slope = lax.dot_general(
+        cotangent, returned_rows, (((1,), (1,)), ((), ())), preferred_element_type=jnp.float32
+    )
+    gate_slope_all = jnp.take_along_axis(token_slot_slope, position, axis=1)
+    centred = gate_slope_all - jnp.sum(gate_weights * gate_slope_all, axis=1, keepdims=True)
+    choice_slope = gate_weights * centred
+    logit_slope = jnp.sum(onehot * choice_slope[:, :, None], axis=1)
+    router_local = jnp.dot(tokens.astype(jnp.float32).T, logit_slope, precision=highest)
+    row_parts = router_local.reshape(owners, model_width // owners, experts_total)
+    row_parts = lax.all_to_all(row_parts, "expert", split_axis=0, concat_axis=0, tiled=True)
+    row_block = lax.psum(jnp.sum(row_parts, axis=0), "dp")
+    row_copies = jnp.broadcast_to(row_block[None], (owners,) + row_block.shape)
+    router_grad = lax.all_to_all(
+        row_copies, "expert", split_axis=0, concat_axis=0, tiled=True
+    ).reshape(model_width, experts_total)
     input_sum = lax.dot_general(
         slot_token_b, back_rows, (((0,), (0,)), ((), ())), preferred_element_type=jnp.float32
     )

time: 799 us -> 851 us (1.065)
  blocking collectives: 195 us -> 23.6 us
  waiting for transfers between devices: 400 us -> 565 us
  starting transfers between devices: 37 us -> 60.7 us
  local copies, waits for them, and re-layouts: 32.5 us -> 55.6 us
  other arithmetic: 26.3 us -> 39.1 us
    all_to_all x2 -> x0, blocking collectives: 171 us -> none  [the longest x1 149 us: shards(): lax.all_to_all(send_slopes, 'expert', split_axis=0, concat_axis=0, tiled=...]
    all_to_all x3, waiting for transfers between devices: 391 us -> 559 us  [the longest x1 280 us: shards(): lax.all_to_all(jnp.concatenate([send_tokens, send_slopes], axis=3), 'expe...]
    all_to_all x3, starting transfers between devices: 30.7 us -> 55.3 us  [the longest x1 24.6 us: shards(): lax.all_to_all(jnp.concatenate([outputs, pick_slope], axis=3), 'expert',...]
    slice x0 -> x2, local copies, waits for them, and re-layouts: none -> 19.7 us  [the longest x1 11.2 us: shards(): received = dispatched[..., :model_width]]
    concatenate x0 -> x2, other arithmetic: none -> 10.6 us  [the longest x1 5.56 us: shards(): jnp.concatenate([send_tokens, send_slopes], axis=3)]
    convert_element_type x2 -> x0, local copies, waits for them, and re-layouts: 9.73 us -> none  [the longest x1 6.55 us: shards(): pick_slope = (jnp.einsum('sjcf,djf->sjcd', expert_gate_slope, gate_full,...]
    all_gather x1, waiting for transfers between devices: 8.86 us -> 0.01 us  [shards(): lax.all_gather(gate_matrix, 'dp', axis=0, tiled=True)]
    unnamed x40 -> x62, local copies, waits for them, and re-layouts: 10.6 us -> 18.1 us
  transfers between devices with their start and end apart: 8 -> 8, of which waited for: 4 -> 4; matrix products, arithmetic and copies ran while one was open for 10% -> 11% of each run, Pallas kernels for 0% -> 0%
where the time goes in v2:
time: 851 us; the launch traced here: 842 us
  waiting for transfers between devices  565 us (66%)
  matrix products  83.7 us (10%)
  starting transfers between devices  60.7 us (7%)
  local copies, waits for them, and re-layouts  55.6 us (7%)
  other arithmetic  39.1 us (5%)
  blocking collectives  23.6 us (3%)
  between operations  14.7 us (2%)
    all_to_all x1, waiting for transfers between devices, shards(): lax.all_to_all(jnp.concatenate([send_tokens, send_slopes], axis=3), 'expe...  280 us
    all_to_all x1, waiting for transfers between devices, shards(): lax.all_to_all(jnp.concatenate([outputs, pick_slope], axis=3), 'expert',...  270 us
    all_to_all x1, starting transfers between devices, shards(): lax.all_to_all(jnp.concatenate([outputs, pick_slope], axis=3), 'expert',...  24.6 us
    psum x1, blocking collectives, shards(): row_block = lax.psum(jnp.sum(row_parts, axis=0), 'dp')  23.6 us
    all_to_all x1, starting transfers between devices, shards(): lax.all_to_all(row_parts, 'expert', split_axis=0, concat_axis=0, tiled=True)  19.2 us
    unnamed x62, local copies, waits for them, and re-layouts  18.1 us
  transfers between devices with their start and end apart: 8, of which 4 were waited for; matrix products, arithmetic and copies ran while one was open for 11% of the time, Pallas kernels for 0%

profile of v2, /device:TPU:32, one launch (start us, length us, event | category | flops | bytes accessed | tf_op | source)
XLA Modules:
  0.0 842.1 jit_solution(5555715088018133139)
XLA Ops:
  13.4 5.6 fusion.1
  19.0 11.5 %select_reduce_fusion = f32[1536]{0:T(1024)S(1)} fusion(f32[128,8]{0,1:T(8,128)S(1)} %exponential_divide_fusion, s32[128,8]{0,1:T(8,128)S(1)} %get-tuple-element.37), kind=kLoop, calls=%fused_computation.12 | loop fusion | flops 4717056 | bytes 14336 | tf_op jit(solution)/shard_map/reduce_sum | solution.py:35
  30.5 2.8 convolution_convert_fusion
  35.1 5.6 pad_maximum_fusion
  40.7 11.5 %all-to-all-start = ((bf16[32,2,24,4096]{3,2,1,0:T(8,128)(2,1)}), bf16[32,2,24,4096]{3,2,1,0:T(8,128)(2,1)}, u32[]{:S(2)}, u32[]{:S(2)}) async-start(bf16[32,2,24,4096]{3,2,1,0:T(8,128)(2,1)} %pad_maximum_fusion), calls=%async_computation | async-start | bytes 25165824 | tf_op jit(solution)/shard_map/all_to_all | solution.py:52
  54.9 280.1 %all-to-all-done = bf16[32,2,24,4096]{3,2,1,0:T(8,128)(2,1)} async-done(((bf16[32,2,24,4096]{3,2,1,0:T(8,128)(2,1)}), bf16[32,2,24,4096]{3,2,1,0:T(8,128)(2,1)}, u32[]{:S(2)}, u32[]{:S(2)}) %all-to-all-start) | async-done | bytes 12582944 | tf_op jit(solution)/shard_map/all_to_all | solution.py:52
  334.9 11.2 %fusion.62 = (bf16[32,2,24,2048]{3,2,1,0:T(8,128)(2,1)}, bf16[32,2,24,2048]{3,2,1,0:T(8,128)(2,1)}) fusion(bf16[32,2,24,4096]{3,2,1,0:T(8,128)(2,1)} %all-to-all-done), kind=kLoop, calls=%fused_computation.90 | loop fusion | bytes 25165824 | tf_op jit(solution)/shard_map/slice | solution.py:59
  346.1 8.6 %fusion.13 = f32[2,32,24,384]{3,2,1,0:T(8,128)} fusion(bf16[32,2,24,2048]{3,2,1,0:T(8,128)(2,1)} %get-tuple-element.40, bf16[2048,2,384]{2,0,1:T(8,128)(2,1)} %all-gather.4.cloned.1.call-done), kind=kOutput, calls=%fused_computation.27 | convolution fusion | flops 2415919104 | bytes 11796480 | tf_op jit(solution)/shard_map/sjcd,djf->sjcf/dot_general | solution.py:61
  354.7 8.6 %fusion.4 = f32[2,32,24,384]{3,2,1,0:T(8,128)} fusion(bf16[32,2,24,2048]{3,2,1,0:T(8,128)(2,1)} %get-tuple-element.41, bf16[2048,2,384]{2,0,1:T(8,128)(2,1)} %all-gather.8.cloned.1.call-done), kind=kOutput, calls=%fused_computation.17 | convolution fusion | flops 2415919104 | bytes 11796480 | tf_op jit(solution)/shard_map/sjcd,djf->sjcf/dot_general | solution.py:68
  363.3 9.4 %fusion.43 = (bf16[32,2,24,384]{3,2,0,1:T(8,128)(2,1)S(1)}, bf16[32,2,24,384]{3,2,0,1:T(8,128)(2,1)S(1)}, bf16[32,2,24,384]{3,2,0,1:T(8,128)(2,1)S(1)}) fusion(f32[2,32,24,384]{3,2,1,0:T(8,128)} %fusion.13, f32[2,32,24,384]{3,2,1,0:T(8,128)} %fusion.4, bf16[2048,2,384]{2,0,1:T(8,128)(2,1)} %all-gather.6.cloned.1.call-done, ...), kind=kOutput, calls=%fused_computation.51 | convolution fusion | flops 2424766464 | bytes 17694720 | tf_op jit(solution)/shard_map/sjcd,djf->sjcf/dot_general | solution.py:62
  372.8 6.4 fusion.23
  379.2 5.4 convert_bitcast_fusion
  384.5 6.6 fusion
  391.2 5.0 pad_maximum_fusion.1
  396.2 5.6 copy.91
  401.8 24.6 %all-to-all-start.1 = ((bf16[32,2,24,4096]{3,2,1,0:T(8,128)(2,1)}), bf16[32,2,24,4096]{3,2,1,0:T(8,128)(2,1)}, u32[]{:S(2)}, u32[]{:S(2)}) async-start(bf16[32,2,24,4096]{3,2,1,0:T(8,128)(2,1)} %copy.91), calls=%async_computation.1 | async-start | bytes 25165824 | tf_op jit(solution)/shard_map/all_to_all | solution.py:84
  426.4 5.4 fusion.28
  431.8 5.5 fusion.31
  437.4 5.5 fusion.34
  442.9 4.4 pad_maximum_fusion.2
  448.1 270.1 %all-to-all-done.1 = bf16[32,2,24,4096]{3,2,1,0:T(8,128)(2,1)} async-done(((bf16[32,2,24,4096]{3,2,1,0:T(8,128)(2,1)}), bf16[32,2,24,4096]{3,2,1,0:T(8,128)(2,1)}, u32[]{:S(2)}, u32[]{:S(2)}) %all-to-all-start.1) | async-done | bytes 12582944 | tf_op jit(solution)/shard_map/all_to_all | solution.py:84
  718.2 8.6 %fusion.61 = (bf16[32,2,24,2048]{3,2,1,0:T(8,128)(2,1)}, bf16[32,2,24,2048]{3,2,1,0:T(8,128)(2,1)S(1)}) fusion(bf16[32,2,24,4096]{3,2,1,0:T(8,128)(2,1)} %all-to-all-done.1), kind=kLoop, calls=%fused_computation.89 | loop fusion | bytes 25165824 | tf_op jit(solution)/shard_map/slice | solution.py:92
  731.3 7.0 gather_fusion
  741.5 19.2 %all-to-all-start.2 = ((f32[32,1,4096]{2,1,0:T(1,128)}), f32[32,1,4096]{2,1,0:T(1,128)S(1)}, u32[]{:S(2)}, u32[]{:S(2)}) async-start(f32[32,1,4096]{2,1,0:T(1,128)} %reshape.115), calls=%async_computation.3 | async-start | bytes 1048576 | tf_op jit(solution)/shard_map/all_to_all | solution.py:109
  765.4 4.8 fusion.64
  770.2 8.3 all-to-all-done.2
  783.7 23.6 %psum.7 = f32[64,64]{0,1:T(8,128)S(1)} all-reduce(f32[64,64]{0,1:T(8,128)S(1)} %bitcast_reduce_fusion), channel_id=1, replica_groups=mesh['dp'=8,'expert'=32] {'dp'}, use_global_device_ids=true, to_apply=%region_9.10 | all-reduce | flops 4096 | bytes 32768 | tf_op jit(solution)/shard_map/psum | solution.py:110
  808.4 2.7 reshape.117
  811.1 5.2 all-to-all-start.3
  816.3 2.9 fusion.38
  819.2 3.9 fusion.51
  825.0 6.1 all-to-all-done.3
  (104 shorter events, 35.8 us)
Async XLA Ops:
  7.2 26.1 %copy-start = (bf16[128,2048]{1,0:T(8,128)(2,1)S(1)}, bf16[128,2048]{1,0:T(8,128)(2,1)}, u32[]{:S(2)}) copy-start(bf16[128,2048]{1,0:T(8,128)(2,1)} %param.13) | copy-start | bytes 1572868
  10.2 0.6 copy-start.12
  13.4 5.6 copy-start.15
  19.0 16.1 %copy-start.2 = (pred[1536,128]{1,0:T(8,128)(4,1)}, pred[1536,128]{1,0:T(8,128)(4,1)S(1)}, u32[]{:S(2)}) copy-start(pred[1536,128]{1,0:T(8,128)(4,1)S(1)} %fusion.1) | copy-start | bytes 589828
  30.5 4.6 copy-start.10
  40.7 11.6 %copy-start.7 = (bf16[256,2,384]{2,1,0:T(2,128)(2,1)S(1)}, bf16[256,2,384]{2,1,0:T(2,128)(2,1)}, u32[]{:S(2)}) copy-start(bf16[256,2,384]{2,1,0:T(2,128)(2,1)} %param.10) | copy-start | bytes 1179652
  40.7 12.5 %copy-start.8 = (bf16[256,2,384]{2,1,0:T(2,128)(2,1)S(1)}, bf16[256,2,384]{2,1,0:T(2,128)(2,1)}, u32[]{:S(2)}) copy-start(bf16[256,2,384]{2,1,0:T(2,128)(2,1)} %param.12) | copy-start | bytes 1179652
  40.7 13.4 %copy-start.9 = (bf16[256,2,384]{2,1,0:T(2,128)(2,1)S(1)}, bf16[256,2,384]{2,1,0:T(2,128)(2,1)}, u32[]{:S(2)}) copy-start(bf16[256,2,384]{2,1,0:T(2,128)(2,1)} %param.11) | copy-start | bytes 1179652
  40.7 294.2 %all-to-all-start = ((bf16[32,2,24,4096]{3,2,1,0:T(8,128)(2,1)}), bf16[32,2,24,4096]{3,2,1,0:T(8,128)(2,1)}, u32[]{:S(2)}, u32[]{:S(2)}) async-start(bf16[32,2,24,4096]{3,2,1,0:T(8,128)(2,1)} %pad_maximum_fusion), calls=%async_computation | async-start | bytes 25165824 | tf_op jit(solution)/shard_map/all_to_all | solution.py:52
  52.2 293.9 %all-gather.4.cloned.1.call-start = ((), (), s32[]{:S(2)}) async-start(), calls=%async_computation.5 | async-start | bytes 3538944 | tf_op jit(solution)/shard_map/all_gather | solution.py:48
  53.1 301.6 %all-gather.8.cloned.1.call-start = ((), (), s32[]{:S(2)}) async-start(), calls=%async_computation.7 | async-start | bytes 3538944 | tf_op jit(solution)/shard_map/all_gather | solution.py:50
  54.0 309.3 %all-gather.6.cloned.1.call-start = ((), (), s32[]{:S(2)}) async-start(), calls=%async_computation.6 | async-start | bytes 3538944 | tf_op jit(solution)/shard_map/all_gather | solution.py:49
  363.3 9.5 %copy-start.5 = (bf16[2048,2,384]{2,0,1:T(8,128)(2,1)S(1)}, bf16[2048,2,384]{2,0,1:T(8,128)(2,1)}, u32[]{:S(2)}) copy-start(bf16[2048,2,384]{2,0,1:T(8,128)(2,1)} %all-gather.4.cloned.1.call-done) | copy-start | bytes 9437188
  372.7 6.4 copy-start.21
  372.8 6.4 copy-start.20
  379.2 5.4 copy-start.6
  401.8 316.5 %all-to-all-start.1 = ((bf16[32,2,24,4096]{3,2,1,0:T(8,128)(2,1)}), bf16[32,2,24,4096]{3,2,1,0:T(8,128)(2,1)}, u32[]{:S(2)}, u32[]{:S(2)}) async-start(bf16[32,2,24,4096]{3,2,1,0:T(8,128)(2,1)} %copy.91), calls=%async_computation.1 | async-start | bytes 25165824 | tf_op jit(solution)/shard_map/all_to_all | solution.py:84
  426.3 334.4 %reduce-scatter.2.cloned.1.call-start = ((), (), s32[]{:S(2)}) async-start(), calls=%async_computation.8 | async-start | bytes 10616832 | tf_op jit(solution)/shard_map/reduce_scatter | solution.py:129
  431.8 5.5 copy-start.22
  447.2 0.7 copy-start.17
  726.8 2.7 copy-start.1
  731.3 7.2 copy-start.13
  731.3 7.2 copy-start.16
  731.3 7.2 copy-start.19
  731.3 7.3 copy-start.14
  731.3 7.3 copy-start.4
  738.4 27.0 %copy-start.3 = (pred[1536,128]{1,0:T(8,128)(4,1)S(1)}, pred[1536,128]{1,0:T(8,128)(4,1)}, u32[]{:S(2)}) copy-start(pred[1536,128]{1,0:T(8,128)(4,1)} %copy-done.2) | copy-start | bytes 589828
  741.5 37.1 %all-to-all-start.2 = ((f32[32,1,4096]{2,1,0:T(1,128)}), f32[32,1,4096]{2,1,0:T(1,128)S(1)}, u32[]{:S(2)}, u32[]{:S(2)}) async-start(f32[32,1,4096]{2,1,0:T(1,128)} %reshape.115), calls=%async_computation.3 | async-start | bytes 1048576 | tf_op jit(solution)/shard_map/all_to_all | solution.py:109
  770.2 49.0 %copy-start.11 = (f32[1536]{0:T(1024)S(1)}, f32[1536]{0:T(1024)}, u32[]{:S(2)}) copy-start(f32[1536]{0:T(1024)} %copy-done.10) | copy-start | bytes 18436
  780.9 42.2 %slice-start = ((s8[6291456]{0:T(1024)(128)(4,1)}), s8[2097152]{0:T(1024)(128)(4,1)S(1)}, s32[]{:S(2)}) async-start(s8[6291456]{0:T(1024)(128)(4,1)} %bitcast.155), calls=%async_computation.9 | async-start | bytes 4194304
  811.1 20.0 %all-to-all-start.3 = ((f32[32,1,4096]{2,1,0:T(1,128)}), f32[32,1,4096]{2,1,0:T(1,128)S(1)}, u32[]{:S(2)}, u32[]{:S(2)}) async-start(f32[32,1,4096]{2,1,0:T(1,128)} %reshape.117), calls=%async_computation.4 | async-start | bytes 1048576 | tf_op jit(solution)/shard_map/all_to_all | solution.py:112
  816.3 6.8 slice-start.1
  (1 other events, 0.5 us)
Sparse Core Ops, SparseCore 0:
  55.4 31.2 all-gather.3
  89.1 30.1 all-gather.7
  121.8 30.1 all-gather.5
  447.4 60.7 reduce-scatter.1

commit v3 on v2

--- a/solution.py
+++ b/solution.py
@@ -49,15 +49,9 @@
         lax.all_gather(up_matrix, "dp", axis=0, tiled=True),
         lax.all_gather(down_matrix, "dp", axis=0, tiled=True),
     )
-    dispatched = lax.all_to_all(
-        jnp.concatenate([send_tokens, send_slopes], axis=3),
-        "expert",
-        split_axis=0,
-        concat_axis=0,
-        tiled=True,
-    )
-    received = dispatched[..., :model_width]
-    slopes_in = dispatched[..., model_width:]
+    received = lax.all_to_all(send_tokens, "expert", split_axis=0, concat_axis=0, tiled=True)
+    received, send_slopes = lax.optimization_barrier((received, send_slopes))
+    slopes_in = lax.all_to_all(send_slopes, "expert", split_axis=0, concat_axis=0, tiled=True)
     pre_gate = jnp.einsum("sjcd,djf->sjcf", received, gate_full, preferred_element_type=jnp.float32)
     pre_up = jnp.einsum("sjcd,djf->sjcf", received, up_full, preferred_element_type=jnp.float32)
     expert_hidden = (jax.nn.silu(pre_gate) * pre_up).astype(jnp.bfloat16)
@@ -65,6 +59,8 @@
         "sjcf,djf->sjcd", expert_hidden, down_full, preferred_element_type=jnp.float32
     ).astype(jnp.bfloat16)
     hidden = expert_hidden
+    outputs, slopes_in = lax.optimization_barrier((outputs, slopes_in))
+    returned = lax.all_to_all(outputs, "expert", split_axis=0, concat_axis=0, tiled=True)
     hidden_slope = jnp.einsum(
         "sjcd,djf->sjcf", slopes_in, down_full, preferred_element_type=jnp.float32
     )
@@ -81,15 +77,9 @@
         + jnp.einsum("sjcf,djf->sjcd", expert_up_slope, up_full, preferred_element_type=jnp.float32)
     ).astype(jnp.bfloat16)
     gate_slope, up_slope = (expert_gate_slope, expert_up_slope)
-    gathered = lax.all_to_all(
-        jnp.concatenate([outputs, pick_slope], axis=3),
-        "expert",
-        split_axis=0,
-        concat_axis=0,
-        tiled=True,
-    )
-    returned_rows = gathered[..., :model_width].reshape(slot_count, model_width)
-    back_rows = gathered[..., model_width:].reshape(slot_count, model_width)
+    pick_slope, returned = lax.optimization_barrier((pick_slope, returned))
+    slopes_back = lax.all_to_all(pick_slope, "expert", split_axis=0, concat_axis=0, tiled=True)
+    returned_rows = returned.reshape(slot_count, model_width)
     slot_mix = jnp.where(slot_token.T, slot_gate[None, :], 0.0)
     mix_high = slot_mix.astype(jnp.bfloat16)
     mix_low = (slot_mix - mix_high.astype(jnp.float32)).astype(jnp.bfloat16)
@@ -112,6 +102,7 @@
     router_grad = lax.all_to_all(
         row_copies, "expert", split_axis=0, concat_axis=0, tiled=True
     ).reshape(model_width, experts_total)
+    back_rows = slopes_back.reshape(slot_count, model_width)
     input_sum = lax.dot_general(
         slot_token_b, back_rows, (((0,), (0,)), ((), ())), preferred_element_type=jnp.float32
     )

time: 851 us -> 731 us (0.86)
  waiting for transfers between devices: 565 us -> 454 us
  blocking collectives: 23.6 us -> 50.2 us
  starting transfers between devices: 60.7 us -> 39.9 us
  local copies, waits for them, and re-layouts: 55.6 us -> 36.5 us
  matrix products: 83.7 us -> 97.3 us
  other arithmetic: 39.1 us -> 26.1 us
    all_to_all x3 -> x4, waiting for transfers between devices: 559 us -> 399 us  [the longest x1 122 us: shards(): lax.all_to_all(send_tokens, 'expert', split_axis=0, concat_axis=0, tiled=...]
    all_to_all x0 -> x1, blocking collectives: none -> 26.6 us  [shards(): lax.all_to_all(row_parts, 'expert', split_axis=0, concat_axis=0, tiled=True)]
    all_gather x1, waiting for transfers between devices: 0.01 us -> 24 us  [shards(): lax.all_gather(up_matrix, 'dp', axis=0, tiled=True)]
    all_gather x1, waiting for transfers between devices: 0.01 us -> 23.3 us  [shards(): lax.all_gather(down_matrix, 'dp', axis=0, tiled=True)]
    all_to_all x3 -> x4, starting transfers between devices: 55.3 us -> 32.4 us  [the longest x1 11.5 us: shards(): lax.all_to_all(send_tokens, 'expert', split_axis=0, concat_axis=0, tiled=...]
    slice x2 -> x0, local copies, waits for them, and re-layouts: 19.7 us -> none  [the longest x1 11.2 us: shards(): received = dispatched[..., :model_width]]
    optimization_barrier x0 -> x2, local copies, waits for them, and re-layouts: none -> 13.1 us  [the longest x1 6.55 us: shards(): pick_slope, returned = lax.optimization_barrier((pick_slope, returned))]
    concatenate x2 -> x0, other arithmetic: 10.6 us -> none  [the longest x1 5.56 us: shards(): jnp.concatenate([send_tokens, send_slopes], axis=3)]
  transfers between devices with their start and end apart: 8 -> 9, of which waited for: 4 -> 7; matrix products, arithmetic and copies ran while one was open for 11% -> 18% of each run, Pallas kernels for 0% -> 0%
where the time goes in v3:
time: 731 us; the launch traced here: 719 us
  waiting for transfers between devices  454 us (62%)
  matrix products  97.3 us (13%)
  blocking collectives  50.2 us (7%)
  starting transfers between devices  39.9 us (5%)
  local copies, waits for them, and re-layouts  36.5 us (5%)
  other arithmetic  26.1 us (4%)
  between operations  14.7 us (2%)
    all_to_all x1, waiting for transfers between devices, shards(): lax.all_to_all(send_tokens, 'expert', split_axis=0, concat_axis=0, tiled=...  122 us
    all_to_all x1, waiting for transfers between devices, shards(): lax.all_to_all(pick_slope, 'expert', split_axis=0, concat_axis=0, tiled=T...  118 us
    all_to_all x1, waiting for transfers between devices, shards(): lax.all_to_all(outputs, 'expert', split_axis=0, concat_axis=0, tiled=True)  93.6 us
    all_to_all x1, waiting for transfers between devices, shards(): lax.all_to_all(send_slopes, 'expert', split_axis=0, concat_axis=0, tiled=...  65.9 us
    all_to_all x1, blocking collectives, shards(): lax.all_to_all(row_parts, 'expert', split_axis=0, concat_axis=0, tiled=True)  26.6 us
    all_gather x1, waiting for transfers between devices, shards(): lax.all_gather(up_matrix, 'dp', axis=0, tiled=True)  24 us
    psum x1, blocking collectives, shards(): row_block = lax.psum(jnp.sum(row_parts, axis=0), 'dp')  23.6 us
    all_gather x1, waiting for transfers between devices, shards(): lax.all_gather(down_matrix, 'dp', axis=0, tiled=True)  23.3 us
  transfers between devices with their start and end apart: 9, of which 7 were waited for; matrix products, arithmetic and copies ran while one was open for 18% of the time, Pallas kernels for 0%

profile of v3, /device:TPU:32, one launch (start us, length us, event | category | flops | bytes accessed | tf_op | source)
XLA Modules:
  0.0 719.0 jit_solution(6669164069288575186)
XLA Ops:
  9.6 5.6 fusion.1
  15.2 5.5 convolution_convert_fusion
  20.7 11.5 %all-to-all-start = ((bf16[32,2,24,2048]{3,2,1,0:T(8,128)(2,1)}), bf16[32,2,24,2048]{3,2,1,0:T(8,128)(2,1)}, u32[]{:S(2)}, u32[]{:S(2)}) async-start(bf16[32,2,24,2048]{3,2,1,0:T(8,128)(2,1)} %bitcast.156), calls=%async_computation | async-start | bytes 12582912 | tf_op jit(solution)/shard_map/all_to_all | solution.py:52
  34.9 11.5 %select_reduce_fusion = f32[1536]{0:T(1024)S(1)} fusion(f32[128,8]{0,1:T(8,128)S(1)} %exponential_divide_fusion, s32[128,8]{0,1:T(8,128)S(1)} %get-tuple-element.49), kind=kLoop, calls=%fused_computation.10 | loop fusion | flops 4717056 | bytes 14336 | tf_op jit(solution)/shard_map/reduce_sum | solution.py:35
  47.0 4.4 multiply_convert_fusion
  51.4 121.7 %all-to-all-done = bf16[32,2,24,2048]{3,2,1,0:T(8,128)(2,1)} async-done(((bf16[32,2,24,2048]{3,2,1,0:T(8,128)(2,1)}), bf16[32,2,24,2048]{3,2,1,0:T(8,128)(2,1)}, u32[]{:S(2)}, u32[]{:S(2)}) %all-to-all-start) | async-done | bytes 6291488 | tf_op jit(solution)/shard_map/all_to_all | solution.py:52
  173.1 8.6 %all-to-all-start.1 = ((bf16[32,2,24,2048]{3,2,1,0:T(8,128)(2,1)}), bf16[32,2,24,2048]{3,2,1,0:T(8,128)(2,1)}, u32[]{:S(2)}, u32[]{:S(2)}) async-start(bf16[32,2,24,2048]{3,2,1,0:T(8,128)(2,1)} %bitcast.155), calls=%async_computation.1 | async-start | bytes 12582912 | tf_op jit(solution)/shard_map/all_to_all | solution.py:54
  184.0 8.5 %fusion.13 = f32[2,32,24,384]{3,2,1,0:T(8,128)} fusion(bf16[32,2,24,2048]{3,2,1,0:T(8,128)(2,1)} %all-to-all-done, bf16[2048,2,384]{2,0,1:T(8,128)(2,1)} %all-gather.4.cloned.1.call-done), kind=kOutput, calls=%fused_computation.25 | convolution fusion | flops 2415919104 | bytes 11796480 | tf_op jit(solution)/shard_map/sjcd,djf->sjcf/dot_general | solution.py:55
  192.5 24.0 %all-gather.6.cloned.1.call-done = bf16[2048,2,384]{2,0,1:T(8,128)(2,1)} async-done(((bf16[256,2,384]{2,0,1:T(8,128)(2,1)}), bf16[2048,2,384]{2,0,1:T(8,128)(2,1)}) %all-gather.6.cloned.1.call-update) | async-done | bytes 3145744 | tf_op jit(solution)/shard_map/all_gather | solution.py:49
  216.5 9.4 %fusion.43 = (bf16[32,2,24,384]{3,2,0,1:T(8,128)(2,1)S(1)}, f32[2,32,24,384]{3,2,1,0:T(8,128)}) fusion(f32[2,32,24,384]{3,2,1,0:T(8,128)} %fusion.13, bf16[2048,2,384]{2,0,1:T(8,128)(2,1)} %all-gather.6.cloned.1.call-done, bf16[32,2,24,2048]{3,2,1,0:T(8,128)(2,1)} %all-to-all-done), kind=kOutput, calls=%fused_computation.49 | convolution fusion | flops 2419458048 | bytes 15335424 | tf_op jit(solution)/shard_map/sjcd,djf->sjcf/dot_general | solution.py:56
  225.9 23.3 %all-gather.8.cloned.1.call-done = bf16[2048,2,384]{2,0,1:T(8,128)(2,1)} async-done(((bf16[256,2,384]{2,0,1:T(8,128)(2,1)}), bf16[2048,2,384]{2,0,1:T(8,128)(2,1)}) %all-gather.8.cloned.1.call-update) | async-done | bytes 3145744 | tf_op jit(solution)/shard_map/all_gather | solution.py:50
  249.1 7.2 %convert_bitcast_fusion = bf16[32,2,24,2048]{3,2,0,1:T(8,128)(2,1)} fusion(bf16[32,2,24,384]{3,2,0,1:T(8,128)(2,1)S(1)} %get-tuple-element.55, bf16[2048,2,384]{2,0,1:T(8,128)(2,1)} %all-gather.8.cloned.1.call-done), kind=kOutput, calls=%fused_computation.9 | convolution fusion | flops 2419064832 | bytes 10616832 | tf_op jit(solution)/shard_map/sjcf,djf->sjcd/dot_general | solution.py:58
  256.4 65.9 %all-to-all-done.1 = bf16[32,2,24,2048]{3,2,1,0:T(8,128)(2,1)} async-done(((bf16[32,2,24,2048]{3,2,1,0:T(8,128)(2,1)}), bf16[32,2,24,2048]{3,2,1,0:T(8,128)(2,1)}, u32[]{:S(2)}, u32[]{:S(2)}) %all-to-all-start.1) | async-done | bytes 6291488 | tf_op jit(solution)/shard_map/all_to_all | solution.py:54
  322.2 6.5 copy.111
  328.8 7.5 %all-to-all-start.2 = ((bf16[32,2,24,2048]{3,2,1,0:T(8,128)(2,1)}), bf16[32,2,24,2048]{3,2,1,0:T(8,128)(2,1)}, u32[]{:S(2)}, u32[]{:S(2)}) async-start(bf16[32,2,24,2048]{3,2,1,0:T(8,128)(2,1)} %copy.111), calls=%async_computation.2 | async-start | bytes 12582912 | tf_op jit(solution)/shard_map/all_to_all | solution.py:63
  336.5 9.2 %fusion.42 = (bf16[32,2,24,384]{3,2,0,1:T(8,128)(2,1)S(1)}, bf16[32,2,24,384]{3,2,0,1:T(8,128)(2,1)S(1)}) fusion(f32[2,32,24,384]{3,2,1,0:T(8,128)} %fusion.13, f32[2,32,24,384]{3,2,1,0:T(8,128)} %get-tuple-element.56, bf16[2048,2,384]{2,0,1:T(8,128)(2,1)} %all-gather.8.cloned.1.call-done, bf16[32,2,24,2048]{3,2,1,0:T(8,128)(2,1)} %all-to-all-done.1), kind=kOutput, calls=%fused_computation.47 | convolution fusion | flops 2423586816 | bytes 16515072 | tf_op jit(solution)/shard_map/sjcd,djf->sjcf/dot_general | solution.py:64
  345.8 5.5 fusion.34
  351.3 5.5 fusion.31
  356.7 5.5 fusion.28
  366.8 8.5 %fusion.23 = f32[2,32,24,2048]{3,2,1,0:T(8,128)} fusion(bf16[32,2,24,384]{3,2,0,1:T(8,128)(2,1)S(1)} %get-tuple-element.51, bf16[2048,2,384]{2,0,1:T(8,128)(2,1)} %all-gather.4.cloned.1.call-done), kind=kOutput, calls=%fused_computation.29 | convolution fusion | flops 2415919104 | bytes 16908288 | tf_op jit(solution)/shard_map/sjcf,djf->sjcd/dot_general | solution.py:74
  375.2 8.4 %fusion = bf16[32,2,24,2048]{3,2,0,1:T(8,128)(2,1)} fusion(f32[2,32,24,2048]{3,2,1,0:T(8,128)} %fusion.23, bf16[32,2,24,384]{3,2,0,1:T(8,128)(2,1)S(1)} %get-tuple-element.50, bf16[2048,2,384]{2,0,1:T(8,128)(2,1)S(1)} %copy-done.5), kind=kOutput, calls=%fused_computation.5 | convolution fusion | flops 2422210560 | bytes 23199744 | tf_op jit(solution)/shard_map/sjcf,djf->sjcd/dot_general | solution.py:77
  383.7 93.6 %all-to-all-done.2 = bf16[32,2,24,2048]{3,2,1,0:T(8,128)(2,1)} async-done(((bf16[32,2,24,2048]{3,2,1,0:T(8,128)(2,1)}), bf16[32,2,24,2048]{3,2,1,0:T(8,128)(2,1)}, u32[]{:S(2)}, u32[]{:S(2)}) %all-to-all-start.2) | async-done | bytes 6291488 | tf_op jit(solution)/shard_map/all_to_all | solution.py:63
  477.2 4.6 convolution_bitcast_fusion
  481.9 7.0 gather_fusion
  491.3 26.6 %all_to_all.30 = f32[32,1,4096]{2,1,0:T(1,128)S(1)} all-to-all(f32[32,1,4096]{2,1,0:T(1,128)S(1)} %reshape.115), channel_id=1, replica_groups=mesh['dp'=8,'expert'=32] {'expert'}, dimensions={0} | all-to-all | bytes 1048576 | tf_op jit(solution)/shard_map/all_to_all | solution.py:99
  520.8 23.6 %psum.7 = f32[64,64]{0,1:T(8,128)S(1)} all-reduce(f32[64,64]{0,1:T(8,128)S(1)} %bitcast_reduce_fusion), channel_id=1, replica_groups=mesh['dp'=8,'expert'=32] {'dp'}, use_global_device_ids=true, to_apply=%region_9.10 | all-reduce | flops 4096 | bytes 32768 | tf_op jit(solution)/shard_map/psum | solution.py:100
  545.9 6.4 all-to-all-start.5
  552.3 6.5 copy.112
  558.9 8.3 %all-to-all-done.5 = f32[32,1,4096]{2,1,0:T(1,128)S(1)} async-done(((f32[32,1,4096]{2,1,0:T(1,128)}), f32[32,1,4096]{2,1,0:T(1,128)S(1)}, u32[]{:S(2)}, u32[]{:S(2)}) %all-to-all-start.5) | async-done | bytes 524320 | tf_op jit(solution)/shard_map/all_to_all | solution.py:102
  567.1 4.7 all-to-all-start.3
  575.8 4.7 fusion.37
  589.1 117.5 %all-to-all-done.3 = bf16[32,2,24,2048]{3,2,1,0:T(8,128)(2,1)} async-done(((bf16[32,2,24,2048]{3,2,1,0:T(8,128)(2,1)}), bf16[32,2,24,2048]{3,2,1,0:T(8,128)(2,1)}, u32[]{:S(2)}, u32[]{:S(2)}) %all-to-all-start.3) | async-done | bytes 6291488 | tf_op jit(solution)/shard_map/all_to_all | solution.py:81
  (99 shorter events, 37.2 us)
Async XLA Ops:
  7.2 39.8 %copy-start = (bf16[128,2048]{1,0:T(8,128)(2,1)S(1)}, bf16[128,2048]{1,0:T(8,128)(2,1)}, u32[]{:S(2)}) copy-start(bf16[128,2048]{1,0:T(8,128)(2,1)} %param.13) | copy-start | bytes 1572868
  9.6 25.3 %copy-start.17 = (s32[128,8]{0,1:T(8,128)}, s32[128,8]{0,1:T(8,128)S(1)}, u32[]{:S(2)}) copy-start(s32[128,8]{0,1:T(8,128)S(1)} %get-tuple-element.49) | copy-start | bytes 12292
  15.2 31.2 %copy-start.1 = (pred[1536,128]{1,0:T(8,128)(4,1)}, pred[1536,128]{1,0:T(8,128)(4,1)S(1)}, u32[]{:S(2)}) copy-start(pred[1536,128]{1,0:T(8,128)(4,1)S(1)} %fusion.1) | copy-start | bytes 589828
  20.7 11.9 %copy-start.8 = (bf16[256,2,384]{2,1,0:T(2,128)(2,1)S(1)}, bf16[256,2,384]{2,1,0:T(2,128)(2,1)}, u32[]{:S(2)}) copy-start(bf16[256,2,384]{2,1,0:T(2,128)(2,1)} %param.10) | copy-start | bytes 1179652
  20.7 12.7 %copy-start.3 = (bf16[128,2048]{1,0:T(8,128)(2,1)S(1)}, bf16[128,2048]{1,0:T(8,128)(2,1)}, u32[]{:S(2)}) copy-start(bf16[128,2048]{1,0:T(8,128)(2,1)} %param.7) | copy-start | bytes 1572868
  20.7 12.7 %copy-start.6 = (bf16[2048,64]{0,1:T(8,128)(2,1)S(1)}, bf16[2048,64]{0,1:T(8,128)(2,1)}, u32[]{:S(2)}) copy-start(bf16[2048,64]{0,1:T(8,128)(2,1)} %param.8) | copy-start | bytes 786436
  20.7 13.1 %copy-start.15 = (s32[128,8]{0,1:T(8,128)S(1)}, s32[128,8]{0,1:T(8,128)}, u32[]{:S(2)}) copy-start(s32[128,8]{0,1:T(8,128)} %param.9) | copy-start | bytes 12292
  20.7 152.3 %all-to-all-start = ((bf16[32,2,24,2048]{3,2,1,0:T(8,128)(2,1)}), bf16[32,2,24,2048]{3,2,1,0:T(8,128)(2,1)}, u32[]{:S(2)}, u32[]{:S(2)}) async-start(bf16[32,2,24,2048]{3,2,1,0:T(8,128)(2,1)} %bitcast.156), calls=%async_computation | async-start | bytes 12582912 | tf_op jit(solution)/shard_map/all_to_all | solution.py:52
  32.3 151.7 %all-gather.4.cloned.1.call-start = ((), (), s32[]{:S(2)}) async-start(), calls=%async_computation.7 | async-start | bytes 3538944 | tf_op jit(solution)/shard_map/all_gather | solution.py:48
  33.8 0.6 copy-start.13
  34.4 0.5 copy-start.19
  46.4 0.6 copy-start.11
  173.1 8.7 %copy-start.9 = (bf16[256,2,384]{2,1,0:T(2,128)(2,1)S(1)}, bf16[256,2,384]{2,1,0:T(2,128)(2,1)}, u32[]{:S(2)}) copy-start(bf16[256,2,384]{2,1,0:T(2,128)(2,1)} %param.11) | copy-start | bytes 1179652
  173.1 10.1 %copy-start.10 = (bf16[256,2,384]{2,1,0:T(2,128)(2,1)S(1)}, bf16[256,2,384]{2,1,0:T(2,128)(2,1)}, u32[]{:S(2)}) copy-start(bf16[256,2,384]{2,1,0:T(2,128)(2,1)} %param.12) | copy-start | bytes 1179652
  173.1 149.2 %all-to-all-start.1 = ((bf16[32,2,24,2048]{3,2,1,0:T(8,128)(2,1)}), bf16[32,2,24,2048]{3,2,1,0:T(8,128)(2,1)}, u32[]{:S(2)}, u32[]{:S(2)}) async-start(bf16[32,2,24,2048]{3,2,1,0:T(8,128)(2,1)} %bitcast.155), calls=%async_computation.1 | async-start | bytes 12582912 | tf_op jit(solution)/shard_map/all_to_all | solution.py:54
  181.7 34.8 %all-gather.6.cloned.1.call-start = ((), (), s32[]{:S(2)}) async-start(), calls=%async_computation.8 | async-start | bytes 3538944 | tf_op jit(solution)/shard_map/all_gather | solution.py:49
  182.6 66.6 %all-gather.8.cloned.1.call-start = ((), (), s32[]{:S(2)}) async-start(), calls=%async_computation.9 | async-start | bytes 3538944 | tf_op jit(solution)/shard_map/all_gather | solution.py:50
  225.9 30.5 %copy-start.21 = (bf16[32,2,24,384]{3,2,0,1:T(8,128)(2,1)}, bf16[32,2,24,384]{3,2,0,1:T(8,128)(2,1)S(1)}, u32[]{:S(2)}) copy-start(bf16[32,2,24,384]{3,2,0,1:T(8,128)(2,1)S(1)} %get-tuple-element.55) | copy-start | bytes 3538948
  328.8 148.4 %all-to-all-start.2 = ((bf16[32,2,24,2048]{3,2,1,0:T(8,128)(2,1)}), bf16[32,2,24,2048]{3,2,1,0:T(8,128)(2,1)}, u32[]{:S(2)}, u32[]{:S(2)}) async-start(bf16[32,2,24,2048]{3,2,1,0:T(8,128)(2,1)} %copy.111), calls=%async_computation.2 | async-start | bytes 12582912 | tf_op jit(solution)/shard_map/all_to_all | solution.py:63
  336.3 248.2 %reduce-scatter.2.cloned.1.call-start = ((), (), s32[]{:S(2)}) async-start(), calls=%async_computation.10 | async-start | bytes 10616832 | tf_op jit(solution)/shard_map/reduce_scatter | solution.py:120
  336.5 9.2 %copy-start.22 = (bf16[32,2,24,384]{3,2,0,1:T(8,128)(2,1)S(1)}, bf16[32,2,24,384]{3,2,0,1:T(8,128)(2,1)}, u32[]{:S(2)}) copy-start(bf16[32,2,24,384]{3,2,0,1:T(8,128)(2,1)} %copy-done.21) | copy-start | bytes 3538948
  366.8 8.5 %copy-start.5 = (bf16[2048,2,384]{2,0,1:T(8,128)(2,1)S(1)}, bf16[2048,2,384]{2,0,1:T(8,128)(2,1)}, u32[]{:S(2)}) copy-start(bf16[2048,2,384]{2,0,1:T(8,128)(2,1)} %all-gather.6.cloned.1.call-done) | copy-start | bytes 9437188
  481.9 7.2 %copy-start.14 = (f32[128,8]{0,1:T(8,128)S(1)}, f32[128,8]{0,1:T(8,128)}, u32[]{:S(2)}) copy-start(f32[128,8]{0,1:T(8,128)} %copy-done.13) | copy-start | bytes 12292
  481.9 7.2 %copy-start.18 = (s32[128,8]{0,1:T(8,128)S(1)}, s32[128,8]{0,1:T(8,128)}, u32[]{:S(2)}) copy-start(s32[128,8]{0,1:T(8,128)} %copy-done.17) | copy-start | bytes 12292
  481.9 7.2 %copy-start.20 = (f32[128]{0:T(128)S(1)}, f32[128]{0:T(128)}, u32[]{:S(2)}) copy-start(f32[128]{0:T(128)} %copy-done.19) | copy-start | bytes 1540
  481.9 7.3 %copy-start.16 = (s32[128,8]{0,1:T(8,128)S(1)}, s32[128,8]{0,1:T(8,128)}, u32[]{:S(2)}) copy-start(s32[128,8]{0,1:T(8,128)} %param.9) | copy-start | bytes 12292
  481.9 7.3 %copy-start.4 = (bf16[128,2048]{1,0:T(8,128)(2,1)S(1)}, bf16[128,2048]{1,0:T(8,128)(2,1)}, u32[]{:S(2)}) copy-start(bf16[128,2048]{1,0:T(8,128)(2,1)} %param.7) | copy-start | bytes 1572868
  545.9 21.2 %all-to-all-start.5 = ((f32[32,1,4096]{2,1,0:T(1,128)}), f32[32,1,4096]{2,1,0:T(1,128)S(1)}, u32[]{:S(2)}, u32[]{:S(2)}) async-start(f32[32,1,4096]{2,1,0:T(1,128)} %reshape.117), calls=%async_computation.6 | async-start | bytes 1048576 | tf_op jit(solution)/shard_map/all_to_all | solution.py:102
  558.9 13.0 %copy-start.2 = (pred[1536,128]{1,0:T(8,128)(4,1)S(1)}, pred[1536,128]{1,0:T(8,128)(4,1)}, u32[]{:S(2)}) copy-start(pred[1536,128]{1,0:T(8,128)(4,1)} %copy-done.1) | copy-start | bytes 589828
  558.9 13.0 %copy-start.12 = (f32[1536]{0:T(1024)S(1)}, f32[1536]{0:T(1024)}, u32[]{:S(2)}) copy-start(f32[1536]{0:T(1024)} %copy-done.11) | copy-start | bytes 18436
  567.1 139.5 %all-to-all-start.3 = ((bf16[32,2,24,2048]{3,2,1,0:T(8,128)(2,1)}), bf16[32,2,24,2048]{3,2,1,0:T(8,128)(2,1)}, u32[]{:S(2)}, u32[]{:S(2)}) async-start(bf16[32,2,24,2048]{3,2,1,0:T(8,128)(2,1)} %copy.112), calls=%async_computation.3 | async-start | bytes 12582912 | tf_op jit(solution)/shard_map/all_to_all | solution.py:81
  706.7 3.9 copy-start.7
Sparse Core Ops, SparseCore 0:
  35.5 31.2 all-gather.3
  184.9 31.5 all-gather.5
  218.9 30.1 all-gather.7
  366.7 61.3 reduce-scatter.1

commit v4 on v3

--- a/solution.py
+++ b/solution.py
@@ -44,11 +44,10 @@
         .astype(jnp.bfloat16)
         .reshape(owners, local_experts, capacity, model_width)
     )
-    gate_full, up_full, down_full = (
-        lax.all_gather(gate_matrix, "dp", axis=0, tiled=True),
-        lax.all_gather(up_matrix, "dp", axis=0, tiled=True),
-        lax.all_gather(down_matrix, "dp", axis=0, tiled=True),
+    weights_full = lax.all_gather(
+        jnp.stack([gate_matrix, up_matrix, down_matrix], axis=0), "dp", axis=1, tiled=True
     )
+    gate_full, up_full, down_full = weights_full[0], weights_full[1], weights_full[2]
     received = lax.all_to_all(send_tokens, "expert", split_axis=0, concat_axis=0, tiled=True)
     received, send_slopes = lax.optimization_barrier((received, send_slopes))
     slopes_in = lax.all_to_all(send_slopes, "expert", split_axis=0, concat_axis=0, tiled=True)

time: 731 us -> 733 us (level)
  matrix products: 97.3 us -> 106 us
  waiting for transfers between devices: 454 us -> 446 us
    all_to_all x1, waiting for transfers between devices: 65.9 us -> 118 us  [shards(): lax.all_to_all(send_slopes, 'expert', split_axis=0, concat_axis=0, tiled=...]
    all_gather x3 -> x1, waiting for transfers between devices: 47.3 us -> 0.02 us  [shards(): lax.all_gather(jnp.stack([gate_matrix, up_matrix, down_matrix], axis=0),...]
    all_to_all x1, waiting for transfers between devices: 93.6 us -> 82.8 us  [shards(): lax.all_to_all(outputs, 'expert', split_axis=0, concat_axis=0, tiled=True)]
  transfers between devices with their start and end apart: 9 -> 7, of which waited for: 7 -> 5; matrix products, arithmetic and copies ran while one was open for 18% -> 20% of each run, Pallas kernels for 0% -> 0%
where the time goes in v4:
time: 733 us; the launch traced here: 722 us
  waiting for transfers between devices  446 us (61%)
  matrix products  106 us (14%)
  blocking collectives  50.6 us (7%)
  starting transfers between devices  39.5 us (5%)
  local copies, waits for them, and re-layouts  37.3 us (5%)
  other arithmetic  27.1 us (4%)
  between operations  14.7 us (2%)
    all_to_all x1, waiting for transfers between devices, shards(): lax.all_to_all(send_tokens, 'expert', split_axis=0, concat_axis=0, tiled=...  122 us
    all_to_all x1, waiting for transfers between devices, shards(): lax.all_to_all(send_slopes, 'expert', split_axis=0, concat_axis=0, tiled=...  118 us
    all_to_all x1, waiting for transfers between devices, shards(): lax.all_to_all(pick_slope, 'expert', split_axis=0, concat_axis=0, tiled=T...  117 us
    all_to_all x1, waiting for transfers between devices, shards(): lax.all_to_all(outputs, 'expert', split_axis=0, concat_axis=0, tiled=True)  82.8 us
    all_to_all x1, blocking collectives, shards(): lax.all_to_all(row_parts, 'expert', split_axis=0, concat_axis=0, tiled=True)  26.6 us
    psum x1, blocking collectives, shards(): row_block = lax.psum(jnp.sum(row_parts, axis=0), 'dp')  24 us
  transfers between devices with their start and end apart: 7, of which 5 were waited for; matrix products, arithmetic and copies ran while one was open for 20% of the time, Pallas kernels for 0%

profile of v4, /device:TPU:32, one launch (start us, length us, event | category | flops | bytes accessed | tf_op | source)
XLA Modules:
  0.0 721.7 jit_solution(5669669920866427193)
XLA Ops:
  9.6 5.6 fusion.1
  15.2 5.6 convolution_convert_fusion
  20.7 11.6 %all-to-all-start = ((bf16[32,2,24,2048]{3,2,1,0:T(8,128)(2,1)}), bf16[32,2,24,2048]{3,2,1,0:T(8,128)(2,1)}, u32[]{:S(2)}, u32[]{:S(2)}) async-start(bf16[32,2,24,2048]{3,2,1,0:T(8,128)(2,1)} %bitcast.163), calls=%async_computation | async-start | bytes 12582912 | tf_op jit(solution)/shard_map/all_to_all | solution.py:51
  34.4 11.5 %select_reduce_fusion = f32[1536]{0:T(1024)S(1)} fusion(f32[128,8]{0,1:T(8,128)S(1)} %exponential_divide_fusion, s32[128,8]{0,1:T(8,128)S(1)} %get-tuple-element.49), kind=kLoop, calls=%fused_computation.10 | loop fusion | flops 4717056 | bytes 14336 | tf_op jit(solution)/shard_map/reduce_sum | solution.py:35
  45.9 4.9 multiply_convert_fusion
  50.7 122.4 %all-to-all-done = bf16[32,2,24,2048]{3,2,1,0:T(8,128)(2,1)} async-done(((bf16[32,2,24,2048]{3,2,1,0:T(8,128)(2,1)}), bf16[32,2,24,2048]{3,2,1,0:T(8,128)(2,1)}, u32[]{:S(2)}, u32[]{:S(2)}) %all-to-all-start) | async-done | bytes 6291488 | tf_op jit(solution)/shard_map/all_to_all | solution.py:51
  173.1 8.6 %all-to-all-start.1 = ((bf16[32,2,24,2048]{3,2,1,0:T(8,128)(2,1)}), bf16[32,2,24,2048]{3,2,1,0:T(8,128)(2,1)}, u32[]{:S(2)}, u32[]{:S(2)}) async-start(bf16[32,2,24,2048]{3,2,1,0:T(8,128)(2,1)} %bitcast.162), calls=%async_computation.1 | async-start | bytes 12582912 | tf_op jit(solution)/shard_map/all_to_all | solution.py:53
  181.8 8.2 %fusion.13 = f32[2,384,32,24]{1,2,3,0:T(8,128)S(1)} fusion(bf16[32,2,24,2048]{3,2,1,0:T(8,128)(2,1)} %all-to-all-done, bf16[3,2048,2,384]{3,1,2,0:T(8,128)(2,1)} %all-gather.2.cloned.1.call-done), kind=kOutput, calls=%fused_computation.25 | convolution fusion | flops 2415919104 | bytes 11796480 | tf_op jit(solution)/shard_map/sjcd,djf->sjcf/dot_general | solution.py:54
  190.0 9.1 %fusion.37 = (bf16[32,2,24,384]{3,0,2,1:T(8,128)(2,1)S(1)}, f32[2,384,32,24]{1,2,3,0:T(8,128)}) fusion(f32[2,384,32,24]{1,2,3,0:T(8,128)S(1)} %fusion.13, bf16[32,2,24,2048]{3,2,1,0:T(8,128)(2,1)} %all-to-all-done, bf16[3,2048,2,384]{3,1,2,0:T(8,128)(2,1)S(1)} %copy-done.4), kind=kOutput, calls=%fused_computation.46 | convolution fusion | flops 2419458048 | bytes 15335424 | tf_op jit(solution)/shard_map/sjcd,djf->sjcf/dot_general | solution.py:55
  199.1 5.3 convert_bitcast_fusion
  204.4 117.7 %all-to-all-done.1 = bf16[32,2,24,2048]{3,2,1,0:T(8,128)(2,1)} async-done(((bf16[32,2,24,2048]{3,2,1,0:T(8,128)(2,1)}), bf16[32,2,24,2048]{3,2,1,0:T(8,128)(2,1)}, u32[]{:S(2)}, u32[]{:S(2)}) %all-to-all-start.1) | async-done | bytes 6291488 | tf_op jit(solution)/shard_map/all_to_all | solution.py:53
  322.1 8.9 %copy.90 = bf16[32,2,24,2048]{3,2,1,0:T(8,128)(2,1)} copy(bf16[32,2,24,2048]{3,0,2,1:T(8,128)(2,1)} %convert_bitcast_fusion) | data formatting | bytes 12582912 | tf_op jit(solution)/shard_map/optimization_barrier | solution.py:61
  331.0 7.6 %all-to-all-start.2 = ((bf16[32,2,24,2048]{3,2,1,0:T(8,128)(2,1)}), bf16[32,2,24,2048]{3,2,1,0:T(8,128)(2,1)}, u32[]{:S(2)}, u32[]{:S(2)}) async-start(bf16[32,2,24,2048]{3,2,1,0:T(8,128)(2,1)} %copy.90), calls=%async_computation.2 | async-start | bytes 12582912 | tf_op jit(solution)/shard_map/all_to_all | solution.py:62
  339.1 9.6 %fusion.36 = (bf16[32,2,24,384]{3,0,2,1:T(8,128)(2,1)S(1)}, bf16[32,2,24,384]{3,0,2,1:T(8,128)(2,1)S(1)}) fusion(f32[2,384,32,24]{1,2,3,0:T(8,128)} %copy-done.16, f32[2,384,32,24]{1,2,3,0:T(8,128)} %get-tuple-element.56, bf16[32,2,24,2048]{3,2,1,0:T(8,128)(2,1)} %all-to-all-done.1, bf16[3,2048,2,384]{3,1,2,0:T(8,128)(2,1)} %all-gather.2.cloned.1.call-done), kind=kOutput, calls=%fused_computation.44 | convolution fusion | flops 2423586816 | bytes 16515072 | tf_op jit(solution)/shard_map/sjcd,djf->sjcf/dot_general | solution.py:63
  348.7 8.0 %fusion.27 = bf16[2048,1,2,384]{0,3,2,1:T(8,128)(2,1)S(1)} fusion(bf16[32,2,24,384]{3,0,2,1:T(8,128)(2,1)S(1)} %copy-done.15, bf16[32,2,24,2048]{3,2,1,0:T(8,128)(2,1)} %all-to-all-done.1), kind=kOutput, calls=%fused_computation.32 | convolution fusion | flops 2417491968 | bytes 10616832 | tf_op jit(solution)/shard_map/sjcd,sjcf->djf/dot_general | solution.py:116
  356.7 7.7 %fusion.24 = bf16[2048,1,2,384]{0,3,2,1:T(8,128)(2,1)S(1)} fusion(bf16[32,2,24,384]{3,0,2,1:T(8,128)(2,1)S(1)} %get-tuple-element.50, bf16[32,2,24,2048]{3,2,1,0:T(8,128)(2,1)} %all-to-all-done), kind=kOutput, calls=%fused_computation.31 | convolution fusion | flops 2417491968 | bytes 10616832 | tf_op jit(solution)/shard_map/sjcd,sjcf->djf/dot_general | solution.py:113
  364.5 7.6 %fusion.21 = bf16[2048,1,2,384]{0,3,2,1:T(8,128)(2,1)S(1)} fusion(bf16[32,2,24,384]{3,0,2,1:T(8,128)(2,1)S(1)} %get-tuple-element.51, bf16[32,2,24,2048]{3,2,1,0:T(8,128)(2,1)} %all-to-all-done), kind=kOutput, calls=%fused_computation.30 | convolution fusion | flops 2417491968 | bytes 10616832 | tf_op jit(solution)/shard_map/sjcd,sjcf->djf/dot_general | solution.py:110
  372.1 4.1 pad_maximum_fusion
  376.4 10.2 %fusion.30 = f32[2,2048,32,24]{1,2,3,0:T(8,128)} fusion(bf16[32,2,24,384]{3,0,2,1:T(8,128)(2,1)} %copy-done.5, bf16[3,2048,2,384]{3,1,2,0:T(8,128)(2,1)} %all-gather.2.cloned.1.call-done), kind=kOutput, calls=%fused_computation.33 | convolution fusion | flops 2415919104 | bytes 16908288 | tf_op jit(solution)/shard_map/sjcf,djf->sjcd/dot_general | solution.py:73
  386.7 10.0 %fusion = bf16[32,2,24,2048]{3,0,2,1:T(8,128)(2,1)} fusion(f32[2,2048,32,24]{1,2,3,0:T(8,128)} %fusion.30, bf16[32,2,24,384]{3,0,2,1:T(8,128)(2,1)S(1)} %get-tuple-element.50, bf16[3,2048,2,384]{3,1,2,0:T(8,128)(2,1)} %all-gather.2.cloned.1.call-done), kind=kOutput, calls=%fused_computation.5 | convolution fusion | flops 2422210560 | bytes 23199744 | tf_op jit(solution)/shard_map/sjcf,djf->sjcd/dot_general | solution.py:76
  396.7 82.8 %all-to-all-done.2 = bf16[32,2,24,2048]{3,2,1,0:T(8,128)(2,1)} async-done(((bf16[32,2,24,2048]{3,2,1,0:T(8,128)(2,1)}), bf16[32,2,24,2048]{3,2,1,0:T(8,128)(2,1)}, u32[]{:S(2)}, u32[]{:S(2)}) %all-to-all-start.2) | async-done | bytes 6291488 | tf_op jit(solution)/shard_map/all_to_all | solution.py:62
  479.5 4.6 convolution_bitcast_fusion
  484.1 7.0 gather_fusion
  493.4 26.6 %all_to_all.30 = f32[32,1,4096]{2,1,0:T(1,128)S(1)} all-to-all(f32[32,1,4096]{2,1,0:T(1,128)S(1)} %reshape.115), channel_id=1, replica_groups=mesh['dp'=8,'expert'=32] {'expert'}, dimensions={0} | all-to-all | bytes 1048576 | tf_op jit(solution)/shard_map/all_to_all | solution.py:98
  522.9 24.0 %psum.7 = f32[64,64]{0,1:T(8,128)S(1)} all-reduce(f32[64,64]{0,1:T(8,128)S(1)} %bitcast_reduce_fusion), channel_id=1, replica_groups=mesh['dp'=8,'expert'=32] {'dp'}, use_global_device_ids=true, to_apply=%region_9.10 | all-reduce | flops 4096 | bytes 32768 | tf_op jit(solution)/shard_map/psum | solution.py:99
  548.5 6.3 all-to-all-start.5
  554.8 8.9 %copy.91 = bf16[32,2,24,2048]{3,2,1,0:T(8,128)(2,1)} copy(bf16[32,2,24,2048]{3,0,2,1:T(8,128)(2,1)} %fusion) | data formatting | bytes 12582912 | tf_op jit(solution)/shard_map/optimization_barrier | solution.py:79
  563.7 6.1 all-to-all-done.5
  569.7 4.7 all-to-all-start.3
  574.5 3.9 fusion.45
  578.4 4.7 fusion.31
  591.8 117.5 %all-to-all-done.3 = bf16[32,2,24,2048]{3,2,1,0:T(8,128)(2,1)} async-done(((bf16[32,2,24,2048]{3,2,1,0:T(8,128)(2,1)}), bf16[32,2,24,2048]{3,2,1,0:T(8,128)(2,1)}, u32[]{:S(2)}, u32[]{:S(2)}) %all-to-all-start.3) | async-done | bytes 6291488 | tf_op jit(solution)/shard_map/all_to_all | solution.py:80
  (81 shorter events, 25.9 us)
Async XLA Ops:
  7.2 38.7 %copy-start = (bf16[128,2048]{1,0:T(8,128)(2,1)S(1)}, bf16[128,2048]{1,0:T(8,128)(2,1)}, u32[]{:S(2)}) copy-start(bf16[128,2048]{1,0:T(8,128)(2,1)} %param.13) | copy-start | bytes 1572868
  15.2 30.7 %copy-start.1 = (pred[1536,128]{1,0:T(8,128)(4,1)}, pred[1536,128]{1,0:T(8,128)(4,1)S(1)}, u32[]{:S(2)}) copy-start(pred[1536,128]{1,0:T(8,128)(4,1)S(1)} %fusion.1) | copy-start | bytes 589828
  20.7 11.8 %copy-start.8 = (bf16[256,2,384]{2,1,0:T(2,128)(2,1)S(1)}, bf16[256,2,384]{2,1,0:T(2,128)(2,1)}, u32[]{:S(2)}) copy-start(bf16[256,2,384]{2,1,0:T(2,128)(2,1)} %param.10) | copy-start | bytes 1179652
  20.7 11.9 %copy-start.9 = (bf16[256,2,384]{2,1,0:T(2,128)(2,1)S(1)}, bf16[256,2,384]{2,1,0:T(2,128)(2,1)}, u32[]{:S(2)}) copy-start(bf16[256,2,384]{2,1,0:T(2,128)(2,1)} %param.12) | copy-start | bytes 1179652
  20.7 11.9 %copy-start.10 = (bf16[256,2,384]{2,1,0:T(2,128)(2,1)S(1)}, bf16[256,2,384]{2,1,0:T(2,128)(2,1)}, u32[]{:S(2)}) copy-start(bf16[256,2,384]{2,1,0:T(2,128)(2,1)} %param.11) | copy-start | bytes 1179652
  20.7 13.2 %copy-start.3 = (bf16[128,2048]{1,0:T(8,128)(2,1)S(1)}, bf16[128,2048]{1,0:T(8,128)(2,1)}, u32[]{:S(2)}) copy-start(bf16[128,2048]{1,0:T(8,128)(2,1)} %param.7) | copy-start | bytes 1572868
  20.7 13.2 %copy-start.6 = (bf16[2048,64]{0,1:T(8,128)(2,1)S(1)}, bf16[2048,64]{0,1:T(8,128)(2,1)}, u32[]{:S(2)}) copy-start(bf16[2048,64]{0,1:T(8,128)(2,1)} %param.8) | copy-start | bytes 786436
  20.7 152.3 %all-to-all-start = ((bf16[32,2,24,2048]{3,2,1,0:T(8,128)(2,1)}), bf16[32,2,24,2048]{3,2,1,0:T(8,128)(2,1)}, u32[]{:S(2)}, u32[]{:S(2)}) async-start(bf16[32,2,24,2048]{3,2,1,0:T(8,128)(2,1)} %bitcast.163), calls=%async_computation | async-start | bytes 12582912 | tf_op jit(solution)/shard_map/all_to_all | solution.py:51
  32.3 2.0 copy-start.13
  32.3 149.5 %all-gather.2.cloned.1.call-start = ((), (), s32[]{:S(2)}) async-start(), calls=%async_computation.7 | async-start | bytes 10616832 | tf_op jit(solution)/shard_map/all_gather | solution.py:47
  45.9 127.2 %copy-start.11 = (f32[1536]{0:T(1024)}, f32[1536]{0:T(1024)S(1)}, u32[]{:S(2)}) copy-start(f32[1536]{0:T(1024)S(1)} %select_reduce_fusion) | copy-start | bytes 18436
  173.1 149.0 %all-to-all-start.1 = ((bf16[32,2,24,2048]{3,2,1,0:T(8,128)(2,1)}), bf16[32,2,24,2048]{3,2,1,0:T(8,128)(2,1)}, u32[]{:S(2)}, u32[]{:S(2)}) async-start(bf16[32,2,24,2048]{3,2,1,0:T(8,128)(2,1)} %bitcast.162), calls=%async_computation.1 | async-start | bytes 12582912 | tf_op jit(solution)/shard_map/all_to_all | solution.py:53
  181.8 8.2 %copy-start.4 = (bf16[3,2048,2,384]{3,1,2,0:T(8,128)(2,1)S(1)}, bf16[3,2048,2,384]{3,1,2,0:T(8,128)(2,1)}, u32[]{:S(2)}) copy-start(bf16[3,2048,2,384]{3,1,2,0:T(8,128)(2,1)} %all-gather.2.cloned.1.call-done) | copy-start | bytes 28311556
  190.0 9.1 %copy-start.16 = (f32[2,384,32,24]{1,2,3,0:T(8,128)}, f32[2,384,32,24]{1,2,3,0:T(8,128)S(1)}, u32[]{:S(2)}) copy-start(f32[2,384,32,24]{1,2,3,0:T(8,128)S(1)} %fusion.13) | copy-start | bytes 7077892
  199.1 5.3 copy-start.14
  331.0 148.5 %all-to-all-start.2 = ((bf16[32,2,24,2048]{3,2,1,0:T(8,128)(2,1)}), bf16[32,2,24,2048]{3,2,1,0:T(8,128)(2,1)}, u32[]{:S(2)}, u32[]{:S(2)}) async-start(bf16[32,2,24,2048]{3,2,1,0:T(8,128)(2,1)} %copy.90), calls=%async_computation.2 | async-start | bytes 12582912 | tf_op jit(solution)/shard_map/all_to_all | solution.py:62
  338.5 248.6 %reduce-scatter.2.cloned.1.call-start = ((), (), s32[]{:S(2)}) async-start(), calls=%async_computation.8 | async-start | bytes 10616832 | tf_op jit(solution)/shard_map/reduce_scatter | solution.py:119
  339.1 9.6 %copy-start.15 = (bf16[32,2,24,384]{3,0,2,1:T(8,128)(2,1)S(1)}, bf16[32,2,24,384]{3,0,2,1:T(8,128)(2,1)}, u32[]{:S(2)}) copy-start(bf16[32,2,24,384]{3,0,2,1:T(8,128)(2,1)} %copy-done.14) | copy-start | bytes 3538948
  348.7 15.8 %copy-start.5 = (bf16[32,2,24,384]{3,0,2,1:T(8,128)(2,1)}, bf16[32,2,24,384]{3,0,2,1:T(8,128)(2,1)S(1)}, u32[]{:S(2)}) copy-start(bf16[32,2,24,384]{3,0,2,1:T(8,128)(2,1)S(1)} %get-tuple-element.51) | copy-start | bytes 3538948
  548.5 21.2 %all-to-all-start.5 = ((f32[32,1,4096]{2,1,0:T(1,128)}), f32[32,1,4096]{2,1,0:T(1,128)S(1)}, u32[]{:S(2)}, u32[]{:S(2)}) async-start(f32[32,1,4096]{2,1,0:T(1,128)} %reshape.117), calls=%async_computation.6 | async-start | bytes 1048576 | tf_op jit(solution)/shard_map/all_to_all | solution.py:101
  563.7 10.8 %copy-start.2 = (pred[1536,128]{1,0:T(8,128)(4,1)S(1)}, pred[1536,128]{1,0:T(8,128)(4,1)}, u32[]{:S(2)}) copy-start(pred[1536,128]{1,0:T(8,128)(4,1)} %copy-done.1) | copy-start | bytes 589828
  563.7 10.8 %copy-start.12 = (f32[1536]{0:T(1024)S(1)}, f32[1536]{0:T(1024)}, u32[]{:S(2)}) copy-start(f32[1536]{0:T(1024)} %copy-done.11) | copy-start | bytes 18436
  569.7 139.5 %all-to-all-start.3 = ((bf16[32,2,24,2048]{3,2,1,0:T(8,128)(2,1)}), bf16[32,2,24,2048]{3,2,1,0:T(8,128)(2,1)}, u32[]{:S(2)}, u32[]{:S(2)}) async-start(bf16[32,2,24,2048]{3,2,1,0:T(8,128)(2,1)} %copy.91), calls=%async_computation.3 | async-start | bytes 12582912 | tf_op jit(solution)/shard_map/all_to_all | solution.py:80
  587.2 126.0 %copy-start.7 = (bf16[2048,64]{0,1:T(8,128)(2,1)S(1)}, bf16[2048,64]{0,1:T(8,128)(2,1)}, u32[]{:S(2)}) copy-start(bf16[2048,64]{0,1:T(8,128)(2,1)} %param.8) | copy-start | bytes 786436
Sparse Core Ops, SparseCore 0:
  35.0 57.6 all-gather.1
  376.4 61.2 reduce-scatter.1

commit v5 on v4

--- a/solution.py
+++ b/solution.py
@@ -94,6 +94,7 @@
     choice_slope = gate_weights * centred
     logit_slope = jnp.sum(onehot * choice_slope[:, :, None], axis=1)
     router_local = jnp.dot(tokens.astype(jnp.float32).T, logit_slope, precision=highest)
+    slopes_back, router_local = lax.optimization_barrier((slopes_back, router_local))
     row_parts = router_local.reshape(owners, model_width // owners, experts_total)
     row_parts = lax.all_to_all(row_parts, "expert", split_axis=0, concat_axis=0, tiled=True)
     row_block = lax.psum(jnp.sum(row_parts, axis=0), "dp")

time: 733 us -> 734 us (level)
  blocking collectives: 50.6 us -> 23.6 us
  waiting for transfers between devices: 446 us -> 466 us
  starting transfers between devices: 39.5 us -> 52.8 us
    all_to_all x1 -> x0, blocking collectives: 26.6 us -> none  [shards(): lax.all_to_all(row_parts, 'expert', split_axis=0, concat_axis=0, tiled=True)]
    all_to_all x0 -> x1, waiting for transfers between devices: none -> 13.8 us  [shards(): lax.all_to_all(row_parts, 'expert', split_axis=0, concat_axis=0, tiled=True)]
    all_to_all x1, waiting for transfers between devices: 117 us -> 128 us  [shards(): lax.all_to_all(pick_slope, 'expert', split_axis=0, concat_axis=0, tiled=T...]
    all_to_all x0 -> x1, starting transfers between devices: none -> 8.94 us  [shards(): lax.all_to_all(row_parts, 'expert', split_axis=0, concat_axis=0, tiled=True)]
  transfers between devices with their start and end apart: 7 -> 8, of which waited for: 5 -> 6; matrix products, arithmetic and copies ran while one was open for 20% -> 19% of each run, Pallas kernels for 0% -> 0%
where the time goes in v5:
time: 734 us; the launch traced here: 728 us
  waiting for transfers between devices  466 us (63%)
  matrix products  103 us (14%)
  starting transfers between devices  52.8 us (7%)
  local copies, waits for them, and re-layouts  41 us (6%)
  other arithmetic  27 us (4%)
  blocking collectives  23.6 us (3%)
  between operations  14.8 us (2%)
    all_to_all x1, waiting for transfers between devices, shards(): lax.all_to_all(pick_slope, 'expert', split_axis=0, concat_axis=0, tiled=T...  128 us
    all_to_all x1, waiting for transfers between devices, shards(): lax.all_to_all(send_tokens, 'expert', split_axis=0, concat_axis=0, tiled=...  121 us
    all_to_all x1, waiting for transfers between devices, shards(): lax.all_to_all(send_slopes, 'expert', split_axis=0, concat_axis=0, tiled=...  117 us
    all_to_all x1, waiting for transfers between devices, shards(): lax.all_to_all(outputs, 'expert', split_axis=0, concat_axis=0, tiled=True)  85.6 us
    psum x1, blocking collectives, shards(): row_block = lax.psum(jnp.sum(row_parts, axis=0), 'dp')  23.6 us
  transfers between devices with their start and end apart: 8, of which 6 were waited for; matrix products, arithmetic and copies ran while one was open for 19% of the time, Pallas kernels for 0%

profile of v5, /device:TPU:32, one launch (start us, length us, event | category | flops | bytes accessed | tf_op | source)
XLA Modules:
  0.0 727.8 jit_solution(9672244088435819442)
XLA Ops:
  9.6 5.6 fusion.1
  15.2 5.5 convolution_convert_fusion
  20.8 11.6 %all-to-all-start = ((bf16[32,2,24,2048]{3,2,1,0:T(8,128)(2,1)}), bf16[32,2,24,2048]{3,2,1,0:T(8,128)(2,1)}, u32[]{:S(2)}, u32[]{:S(2)}) async-start(bf16[32,2,24,2048]{3,2,1,0:T(8,128)(2,1)} %bitcast.163), calls=%async_computation | async-start | bytes 12582912 | tf_op jit(solution)/shard_map/all_to_all | solution.py:51
  35.5 11.5 %select_reduce_fusion = f32[1536]{0:T(1024)S(1)} fusion(f32[128,8]{0,1:T(8,128)S(1)} %exponential_divide_fusion, s32[128,8]{0,1:T(8,128)S(1)} %get-tuple-element.53), kind=kLoop, calls=%fused_computation.10 | loop fusion | flops 4717056 | bytes 14336 | tf_op jit(solution)/shard_map/reduce_sum | solution.py:35
  47.5 4.6 multiply_convert_fusion
  52.2 120.9 %all-to-all-done = bf16[32,2,24,2048]{3,2,1,0:T(8,128)(2,1)} async-done(((bf16[32,2,24,2048]{3,2,1,0:T(8,128)(2,1)}), bf16[32,2,24,2048]{3,2,1,0:T(8,128)(2,1)}, u32[]{:S(2)}, u32[]{:S(2)}) %all-to-all-start) | async-done | bytes 6291488 | tf_op jit(solution)/shard_map/all_to_all | solution.py:51
  173.1 9.1 %all-to-all-start.1 = ((bf16[32,2,24,2048]{3,2,1,0:T(8,128)(2,1)}), bf16[32,2,24,2048]{3,2,1,0:T(8,128)(2,1)}, u32[]{:S(2)}, u32[]{:S(2)}) async-start(bf16[32,2,24,2048]{3,2,1,0:T(8,128)(2,1)} %bitcast.162), calls=%async_computation.1 | async-start | bytes 12582912 | tf_op jit(solution)/shard_map/all_to_all | solution.py:53
  182.3 8.2 %fusion.13 = f32[2,384,32,24]{1,2,3,0:T(8,128)S(1)} fusion(bf16[32,2,24,2048]{3,2,1,0:T(8,128)(2,1)} %all-to-all-done, bf16[3,2048,2,384]{3,1,2,0:T(8,128)(2,1)} %all-gather.2.cloned.1.call-done), kind=kOutput, calls=%fused_computation.25 | convolution fusion | flops 2415919104 | bytes 11796480 | tf_op jit(solution)/shard_map/sjcd,djf->sjcf/dot_general | solution.py:54
  190.5 9.1 %fusion.37 = (bf16[32,2,24,384]{3,0,2,1:T(8,128)(2,1)S(1)}, f32[2,384,32,24]{1,2,3,0:T(8,128)}) fusion(f32[2,384,32,24]{1,2,3,0:T(8,128)S(1)} %fusion.13, bf16[32,2,24,2048]{3,2,1,0:T(8,128)(2,1)} %all-to-all-done, bf16[3,2048,2,384]{3,1,2,0:T(8,128)(2,1)S(1)} %copy-done.5), kind=kOutput, calls=%fused_computation.46 | convolution fusion | flops 2419458048 | bytes 15335424 | tf_op jit(solution)/shard_map/sjcd,djf->sjcf/dot_general | solution.py:55
  200.6 5.3 convert_bitcast_fusion
  205.9 116.6 %all-to-all-done.1 = bf16[32,2,24,2048]{3,2,1,0:T(8,128)(2,1)} async-done(((bf16[32,2,24,2048]{3,2,1,0:T(8,128)(2,1)}), bf16[32,2,24,2048]{3,2,1,0:T(8,128)(2,1)}, u32[]{:S(2)}, u32[]{:S(2)}) %all-to-all-start.1) | async-done | bytes 6291488 | tf_op jit(solution)/shard_map/all_to_all | solution.py:53
  322.5 8.9 %copy.90 = bf16[32,2,24,2048]{3,2,1,0:T(8,128)(2,1)} copy(bf16[32,2,24,2048]{3,0,2,1:T(8,128)(2,1)} %convert_bitcast_fusion) | data formatting | bytes 12582912 | tf_op jit(solution)/shard_map/optimization_barrier | solution.py:61
  331.3 7.7 %all-to-all-start.2 = ((bf16[32,2,24,2048]{3,2,1,0:T(8,128)(2,1)}), bf16[32,2,24,2048]{3,2,1,0:T(8,128)(2,1)}, u32[]{:S(2)}, u32[]{:S(2)}) async-start(bf16[32,2,24,2048]{3,2,1,0:T(8,128)(2,1)} %copy.90), calls=%async_computation.2 | async-start | bytes 12582912 | tf_op jit(solution)/shard_map/all_to_all | solution.py:62
  339.5 9.6 %fusion.36 = (bf16[32,2,24,384]{3,0,2,1:T(8,128)(2,1)S(1)}, bf16[32,2,24,384]{3,0,2,1:T(8,128)(2,1)S(1)}) fusion(f32[2,384,32,24]{1,2,3,0:T(8,128)} %copy-done.23, f32[2,384,32,24]{1,2,3,0:T(8,128)} %get-tuple-element.60, bf16[32,2,24,2048]{3,2,1,0:T(8,128)(2,1)} %all-to-all-done.1, bf16[3,2048,2,384]{3,1,2,0:T(8,128)(2,1)} %all-gather.2.cloned.1.call-done), kind=kOutput, calls=%fused_computation.44 | convolution fusion | flops 2423586816 | bytes 16515072 | tf_op jit(solution)/shard_map/sjcd,djf->sjcf/dot_general | solution.py:63
  349.2 7.6 %fusion.27 = bf16[2048,1,2,384]{0,3,2,1:T(8,128)(2,1)S(1)} fusion(bf16[32,2,24,384]{3,0,2,1:T(8,128)(2,1)S(1)} %copy-done.22, bf16[32,2,24,2048]{3,2,1,0:T(8,128)(2,1)} %all-to-all-done.1), kind=kOutput, calls=%fused_computation.32 | convolution fusion | flops 2417491968 | bytes 10616832 | tf_op jit(solution)/shard_map/sjcd,sjcf->djf/dot_general | solution.py:117
  356.8 7.7 %fusion.24 = bf16[2048,1,2,384]{0,3,2,1:T(8,128)(2,1)S(1)} fusion(bf16[32,2,24,384]{3,0,2,1:T(8,128)(2,1)S(1)} %get-tuple-element.54, bf16[32,2,24,2048]{3,2,1,0:T(8,128)(2,1)} %all-to-all-done), kind=kOutput, calls=%fused_computation.31 | convolution fusion | flops 2417491968 | bytes 10616832 | tf_op jit(solution)/shard_map/sjcd,sjcf->djf/dot_general | solution.py:114
  364.5 7.5 %fusion.21 = bf16[2048,1,2,384]{0,3,2,1:T(8,128)(2,1)S(1)} fusion(bf16[32,2,24,384]{3,0,2,1:T(8,128)(2,1)S(1)} %get-tuple-element.55, bf16[32,2,24,2048]{3,2,1,0:T(8,128)(2,1)} %all-to-all-done), kind=kOutput, calls=%fused_computation.30 | convolution fusion | flops 2417491968 | bytes 10616832 | tf_op jit(solution)/shard_map/sjcd,sjcf->djf/dot_general | solution.py:111
  372.0 4.1 pad_maximum_fusion
  376.2 8.2 %fusion.30 = f32[2,2048,32,24]{1,2,3,0:T(8,128)} fusion(bf16[32,2,24,384]{3,0,2,1:T(8,128)(2,1)S(1)} %get-tuple-element.55, bf16[3,2048,2,384]{3,1,2,0:T(8,128)(2,1)} %all-gather.2.cloned.1.call-done), kind=kOutput, calls=%fused_computation.33 | convolution fusion | flops 2415919104 | bytes 16908288 | tf_op jit(solution)/shard_map/sjcf,djf->sjcd/dot_general | solution.py:73
  384.4 9.9 %fusion = bf16[32,2,24,2048]{3,0,2,1:T(8,128)(2,1)} fusion(f32[2,2048,32,24]{1,2,3,0:T(8,128)} %fusion.30, bf16[32,2,24,384]{3,0,2,1:T(8,128)(2,1)S(1)} %get-tuple-element.54, bf16[3,2048,2,384]{3,1,2,0:T(8,128)(2,1)} %all-gather.2.cloned.1.call-done), kind=kOutput, calls=%fused_computation.5 | convolution fusion | flops 2422210560 | bytes 23199744 | tf_op jit(solution)/shard_map/sjcf,djf->sjcd/dot_general | solution.py:76
  394.3 85.6 %all-to-all-done.2 = bf16[32,2,24,2048]{3,2,1,0:T(8,128)(2,1)} async-done(((bf16[32,2,24,2048]{3,2,1,0:T(8,128)(2,1)}), bf16[32,2,24,2048]{3,2,1,0:T(8,128)(2,1)}, u32[]{:S(2)}, u32[]{:S(2)}) %all-to-all-start.2) | async-done | bytes 6291488 | tf_op jit(solution)/shard_map/all_to_all | solution.py:62
  479.9 8.9 %copy.91 = bf16[32,2,24,2048]{3,2,1,0:T(8,128)(2,1)} copy(bf16[32,2,24,2048]{3,0,2,1:T(8,128)(2,1)} %fusion) | data formatting | bytes 12582912 | tf_op jit(solution)/shard_map/optimization_barrier | solution.py:79
  488.8 9.1 %all-to-all-start.3 = ((bf16[32,2,24,2048]{3,2,1,0:T(8,128)(2,1)}), bf16[32,2,24,2048]{3,2,1,0:T(8,128)(2,1)}, u32[]{:S(2)}, u32[]{:S(2)}) async-start(bf16[32,2,24,2048]{3,2,1,0:T(8,128)(2,1)} %copy.91), calls=%async_computation.3 | async-start | bytes 12582912 | tf_op jit(solution)/shard_map/all_to_all | solution.py:80
  498.1 4.6 convolution_bitcast_fusion
  502.8 7.0 gather_fusion
  510.5 128.3 %all-to-all-done.3 = bf16[32,2,24,2048]{3,2,1,0:T(8,128)(2,1)} async-done(((bf16[32,2,24,2048]{3,2,1,0:T(8,128)(2,1)}), bf16[32,2,24,2048]{3,2,1,0:T(8,128)(2,1)}, u32[]{:S(2)}, u32[]{:S(2)}) %all-to-all-start.3) | async-done | bytes 6291488 | tf_op jit(solution)/shard_map/all_to_all | solution.py:80
  641.3 8.9 %all-to-all-start.4 = ((f32[32,1,4096]{2,1,0:T(1,128)}), f32[32,1,4096]{2,1,0:T(1,128)S(1)}, u32[]{:S(2)}, u32[]{:S(2)}) async-start(f32[32,1,4096]{2,1,0:T(1,128)} %reshape.115), calls=%async_computation.5 | async-start | bytes 1048576 | tf_op jit(solution)/shard_map/all_to_all | solution.py:99
  650.2 3.9 fusion.45
  654.1 13.8 %all-to-all-done.4 = f32[32,1,4096]{2,1,0:T(1,128)S(1)} async-done(((f32[32,1,4096]{2,1,0:T(1,128)}), f32[32,1,4096]{2,1,0:T(1,128)S(1)}, u32[]{:S(2)}, u32[]{:S(2)}) %all-to-all-start.4) | async-done | bytes 524320 | tf_op jit(solution)/shard_map/all_to_all | solution.py:99
  670.8 23.6 %psum.7 = f32[64,64]{0,1:T(8,128)S(1)} all-reduce(f32[64,64]{0,1:T(8,128)S(1)} %bitcast_reduce_fusion), channel_id=1, replica_groups=mesh['dp'=8,'expert'=32] {'dp'}, use_global_device_ids=true, to_apply=%region_9.10 | all-reduce | flops 4096 | bytes 32768 | tf_op jit(solution)/shard_map/psum | solution.py:100
  696.0 5.8 all-to-all-start.5
  701.7 4.7 fusion.31
  (96 shorter events, 29.7 us)
Async XLA Ops:
  7.2 40.4 %copy-start = (bf16[128,2048]{1,0:T(8,128)(2,1)S(1)}, bf16[128,2048]{1,0:T(8,128)(2,1)}, u32[]{:S(2)}) copy-start(bf16[128,2048]{1,0:T(8,128)(2,1)} %param.13) | copy-start | bytes 1572868
  9.6 25.9 %copy-start.17 = (s32[128,8]{0,1:T(8,128)}, s32[128,8]{0,1:T(8,128)S(1)}, u32[]{:S(2)}) copy-start(s32[128,8]{0,1:T(8,128)S(1)} %get-tuple-element.53) | copy-start | bytes 12292
  15.2 31.8 %copy-start.1 = (pred[1536,128]{1,0:T(8,128)(4,1)}, pred[1536,128]{1,0:T(8,128)(4,1)S(1)}, u32[]{:S(2)}) copy-start(pred[1536,128]{1,0:T(8,128)(4,1)S(1)} %fusion.1) | copy-start | bytes 589828
  20.7 11.8 %copy-start.8 = (bf16[256,2,384]{2,1,0:T(2,128)(2,1)S(1)}, bf16[256,2,384]{2,1,0:T(2,128)(2,1)}, u32[]{:S(2)}) copy-start(bf16[256,2,384]{2,1,0:T(2,128)(2,1)} %param.10) | copy-start | bytes 1179652
  20.7 11.9 %copy-start.9 = (bf16[256,2,384]{2,1,0:T(2,128)(2,1)S(1)}, bf16[256,2,384]{2,1,0:T(2,128)(2,1)}, u32[]{:S(2)}) copy-start(bf16[256,2,384]{2,1,0:T(2,128)(2,1)} %param.12) | copy-start | bytes 1179652
  20.7 11.9 %copy-start.10 = (bf16[256,2,384]{2,1,0:T(2,128)(2,1)S(1)}, bf16[256,2,384]{2,1,0:T(2,128)(2,1)}, u32[]{:S(2)}) copy-start(bf16[256,2,384]{2,1,0:T(2,128)(2,1)} %param.11) | copy-start | bytes 1179652
  20.7 13.2 %copy-start.3 = (bf16[128,2048]{1,0:T(8,128)(2,1)S(1)}, bf16[128,2048]{1,0:T(8,128)(2,1)}, u32[]{:S(2)}) copy-start(bf16[128,2048]{1,0:T(8,128)(2,1)} %param.7) | copy-start | bytes 1572868
  20.7 13.3 %copy-start.6 = (bf16[2048,64]{0,1:T(8,128)(2,1)S(1)}, bf16[2048,64]{0,1:T(8,128)(2,1)}, u32[]{:S(2)}) copy-start(bf16[2048,64]{0,1:T(8,128)(2,1)} %param.8) | copy-start | bytes 786436
  20.8 152.3 %all-to-all-start = ((bf16[32,2,24,2048]{3,2,1,0:T(8,128)(2,1)}), bf16[32,2,24,2048]{3,2,1,0:T(8,128)(2,1)}, u32[]{:S(2)}, u32[]{:S(2)}) async-start(bf16[32,2,24,2048]{3,2,1,0:T(8,128)(2,1)} %bitcast.163), calls=%async_computation | async-start | bytes 12582912 | tf_op jit(solution)/shard_map/all_to_all | solution.py:51
  32.3 2.0 copy-start.15
  32.3 149.9 %all-gather.2.cloned.1.call-start = ((), (), s32[]{:S(2)}) async-start(), calls=%async_computation.7 | async-start | bytes 10616832 | tf_op jit(solution)/shard_map/all_gather | solution.py:47
  34.4 0.6 copy-start.13
  35.0 0.5 copy-start.19
  46.9 0.6 copy-start.11
  173.1 149.4 %all-to-all-start.1 = ((bf16[32,2,24,2048]{3,2,1,0:T(8,128)(2,1)}), bf16[32,2,24,2048]{3,2,1,0:T(8,128)(2,1)}, u32[]{:S(2)}, u32[]{:S(2)}) async-start(bf16[32,2,24,2048]{3,2,1,0:T(8,128)(2,1)} %bitcast.162), calls=%async_computation.1 | async-start | bytes 12582912 | tf_op jit(solution)/shard_map/all_to_all | solution.py:53
  182.2 8.2 %copy-start.5 = (bf16[3,2048,2,384]{3,1,2,0:T(8,128)(2,1)S(1)}, bf16[3,2048,2,384]{3,1,2,0:T(8,128)(2,1)}, u32[]{:S(2)}) copy-start(bf16[3,2048,2,384]{3,1,2,0:T(8,128)(2,1)} %all-gather.2.cloned.1.call-done) | copy-start | bytes 28311556
  190.5 9.1 %copy-start.23 = (f32[2,384,32,24]{1,2,3,0:T(8,128)}, f32[2,384,32,24]{1,2,3,0:T(8,128)S(1)}, u32[]{:S(2)}) copy-start(f32[2,384,32,24]{1,2,3,0:T(8,128)S(1)} %fusion.13) | copy-start | bytes 7077892
  199.5 1.1 copy-start.21
  331.3 148.6 %all-to-all-start.2 = ((bf16[32,2,24,2048]{3,2,1,0:T(8,128)(2,1)}), bf16[32,2,24,2048]{3,2,1,0:T(8,128)(2,1)}, u32[]{:S(2)}, u32[]{:S(2)}) async-start(bf16[32,2,24,2048]{3,2,1,0:T(8,128)(2,1)} %copy.90), calls=%async_computation.2 | async-start | bytes 12582912 | tf_op jit(solution)/shard_map/all_to_all | solution.py:62
  339.0 367.4 %reduce-scatter.2.cloned.1.call-start = ((), (), s32[]{:S(2)}) async-start(), calls=%async_computation.8 | async-start | bytes 10616832 | tf_op jit(solution)/shard_map/reduce_scatter | solution.py:120
  339.5 9.6 %copy-start.22 = (bf16[32,2,24,384]{3,0,2,1:T(8,128)(2,1)S(1)}, bf16[32,2,24,384]{3,0,2,1:T(8,128)(2,1)}, u32[]{:S(2)}) copy-start(bf16[32,2,24,384]{3,0,2,1:T(8,128)(2,1)} %copy-done.21) | copy-start | bytes 3538948
  488.8 150.0 %all-to-all-start.3 = ((bf16[32,2,24,2048]{3,2,1,0:T(8,128)(2,1)}), bf16[32,2,24,2048]{3,2,1,0:T(8,128)(2,1)}, u32[]{:S(2)}, u32[]{:S(2)}) async-start(bf16[32,2,24,2048]{3,2,1,0:T(8,128)(2,1)} %copy.91), calls=%async_computation.3 | async-start | bytes 12582912 | tf_op jit(solution)/shard_map/all_to_all | solution.py:80
  502.7 7.3 copy-start.14
  502.7 7.2 copy-start.18
  502.8 7.2 copy-start.20
  502.8 7.3 %copy-start.16 = (s32[128,8]{0,1:T(8,128)S(1)}, s32[128,8]{0,1:T(8,128)}, u32[]{:S(2)}) copy-start(s32[128,8]{0,1:T(8,128)} %param.9) | copy-start | bytes 12292
  502.8 7.3 %copy-start.4 = (bf16[128,2048]{1,0:T(8,128)(2,1)S(1)}, bf16[128,2048]{1,0:T(8,128)(2,1)}, u32[]{:S(2)}) copy-start(bf16[128,2048]{1,0:T(8,128)(2,1)} %param.7) | copy-start | bytes 1572868
  509.8 140.4 %copy-start.2 = (pred[1536,128]{1,0:T(8,128)(4,1)S(1)}, pred[1536,128]{1,0:T(8,128)(4,1)}, u32[]{:S(2)}) copy-start(pred[1536,128]{1,0:T(8,128)(4,1)} %copy-done.1) | copy-start | bytes 589828
  509.8 140.4 %copy-start.12 = (f32[1536]{0:T(1024)S(1)}, f32[1536]{0:T(1024)}, u32[]{:S(2)}) copy-start(f32[1536]{0:T(1024)} %copy-done.11) | copy-start | bytes 18436
  641.3 26.6 %all-to-all-start.4 = ((f32[32,1,4096]{2,1,0:T(1,128)}), f32[32,1,4096]{2,1,0:T(1,128)S(1)}, u32[]{:S(2)}, u32[]{:S(2)}) async-start(f32[32,1,4096]{2,1,0:T(1,128)} %reshape.115), calls=%async_computation.5 | async-start | bytes 1048576 | tf_op jit(solution)/shard_map/all_to_all | solution.py:99
  696.0 20.7 %all-to-all-start.5 = ((f32[32,1,4096]{2,1,0:T(1,128)}), f32[32,1,4096]{2,1,0:T(1,128)S(1)}, u32[]{:S(2)}, u32[]{:S(2)}) async-start(f32[32,1,4096]{2,1,0:T(1,128)} %reshape.117), calls=%async_computation.6 | async-start | bytes 1048576 | tf_op jit(solution)/shard_map/all_to_all | solution.py:102
  706.4 8.5 %copy-start.7 = (bf16[2048,64]{0,1:T(8,128)(2,1)S(1)}, bf16[2048,64]{0,1:T(8,128)(2,1)}, u32[]{:S(2)}) copy-start(bf16[2048,64]{0,1:T(8,128)(2,1)} %param.8) | copy-start | bytes 786436
Sparse Core Ops, SparseCore 0:
  35.0 57.6 all-gather.1
  376.3 61.0 reduce-scatter.1

commit v6 on v4

--- a/solution.py
+++ b/solution.py
@@ -94,9 +94,11 @@
     choice_slope = gate_weights * centred
     logit_slope = jnp.sum(onehot * choice_slope[:, :, None], axis=1)
     router_local = jnp.dot(tokens.astype(jnp.float32).T, logit_slope, precision=highest)
-    row_parts = router_local.reshape(owners, model_width // owners, experts_total)
+    router_group = lax.psum(router_local, "dp")
+    slopes_back, router_group = lax.optimization_barrier((slopes_back, router_group))
+    row_parts = router_group.reshape(owners, model_width // owners, experts_total)
     row_parts = lax.all_to_all(row_parts, "expert", split_axis=0, concat_axis=0, tiled=True)
-    row_block = lax.psum(jnp.sum(row_parts, axis=0), "dp")
+    row_block = jnp.sum(row_parts, axis=0)
     row_copies = jnp.broadcast_to(row_block[None], (owners,) + row_block.shape)
     router_grad = lax.all_to_all(
         row_copies, "expert", split_axis=0, concat_axis=0, tiled=True

time: 733 us -> 735 us (level)
  blocking collectives: 50.6 us -> 0 us
  waiting for transfers between devices: 446 us -> 482 us
  starting transfers between devices: 39.5 us -> 52.2 us
    psum x0 -> x1, waiting for transfers between devices: none -> 40.5 us  [shards(): router_group = lax.psum(router_local, 'dp')]
    all_to_all x1 -> x0, blocking collectives: 26.6 us -> none  [shards(): lax.all_to_all(row_parts, 'expert', split_axis=0, concat_axis=0, tiled=True)]
    psum x1 -> x0, blocking collectives: 24 us -> none  [shards(): row_block = lax.psum(jnp.sum(row_parts, axis=0), 'dp')]
    all_to_all x1, waiting for transfers between devices: 117 us -> 100 us  [shards(): lax.all_to_all(pick_slope, 'expert', split_axis=0, concat_axis=0, tiled=T...]
    all_to_all x0 -> x1, waiting for transfers between devices: none -> 13.6 us  [shards(): lax.all_to_all(row_parts, 'expert', split_axis=0, concat_axis=0, tiled=True)]
    all_to_all x0 -> x1, starting transfers between devices: none -> 9.53 us  [shards(): lax.all_to_all(row_parts, 'expert', split_axis=0, concat_axis=0, tiled=True)]
  transfers between devices with their start and end apart: 7 -> 9, of which waited for: 5 -> 7; matrix products, arithmetic and copies ran while one was open for 20% -> 19% of each run, Pallas kernels for 0% -> 0%
where the time goes in v6:
time: 735 us; the launch traced here: 729 us
  waiting for transfers between devices  482 us (66%)
  matrix products  109 us (15%)
  starting transfers between devices  52.2 us (7%)
  local copies, waits for them, and re-layouts  39.2 us (5%)
  other arithmetic  32 us (4%)
  between operations  14.6 us (2%)
    all_to_all x1, waiting for transfers between devices, shards(): lax.all_to_all(send_tokens, 'expert', split_axis=0, concat_axis=0, tiled=...  122 us
    all_to_all x1, waiting for transfers between devices, shards(): lax.all_to_all(send_slopes, 'expert', split_axis=0, concat_axis=0, tiled=...  118 us
    all_to_all x1, waiting for transfers between devices, shards(): lax.all_to_all(pick_slope, 'expert', split_axis=0, concat_axis=0, tiled=T...  100 us
    all_to_all x1, waiting for transfers between devices, shards(): lax.all_to_all(outputs, 'expert', split_axis=0, concat_axis=0, tiled=True)  85.6 us
    psum x1, waiting for transfers between devices, shards(): router_group = lax.psum(router_local, 'dp')  40.5 us
  transfers between devices with their start and end apart: 9, of which 7 were waited for; matrix products, arithmetic and copies ran while one was open for 19% of the time, Pallas kernels for 0%

profile of v6, /device:TPU:32, one launch (start us, length us, event | category | flops | bytes accessed | tf_op | source)
XLA Modules:
  0.0 729.0 jit_solution(3661028450269492863)
XLA Ops:
  9.6 5.6 fusion.1
  15.2 5.5 convolution_convert_fusion
  20.7 11.5 %all-to-all-start = ((bf16[32,2,24,2048]{3,2,1,0:T(8,128)(2,1)}), bf16[32,2,24,2048]{3,2,1,0:T(8,128)(2,1)}, u32[]{:S(2)}, u32[]{:S(2)}) async-start(bf16[32,2,24,2048]{3,2,1,0:T(8,128)(2,1)} %bitcast.163), calls=%async_computation | async-start | bytes 12582912 | tf_op jit(solution)/shard_map/all_to_all | solution.py:51
  34.4 11.5 %select_reduce_fusion = f32[1536]{0:T(1024)S(1)} fusion(f32[128,8]{0,1:T(8,128)S(1)} %exponential_divide_fusion, s32[128,8]{0,1:T(8,128)S(1)} %get-tuple-element.53), kind=kLoop, calls=%fused_computation.10 | loop fusion | flops 4717056 | bytes 14336 | tf_op jit(solution)/shard_map/reduce_sum | solution.py:35
  45.9 4.9 multiply_convert_fusion
  50.7 122.4 %all-to-all-done = bf16[32,2,24,2048]{3,2,1,0:T(8,128)(2,1)} async-done(((bf16[32,2,24,2048]{3,2,1,0:T(8,128)(2,1)}), bf16[32,2,24,2048]{3,2,1,0:T(8,128)(2,1)}, u32[]{:S(2)}, u32[]{:S(2)}) %all-to-all-start) | async-done | bytes 6291488 | tf_op jit(solution)/shard_map/all_to_all | solution.py:51
  173.1 9.2 %all-to-all-start.1 = ((bf16[32,2,24,2048]{3,2,1,0:T(8,128)(2,1)}), bf16[32,2,24,2048]{3,2,1,0:T(8,128)(2,1)}, u32[]{:S(2)}, u32[]{:S(2)}) async-start(bf16[32,2,24,2048]{3,2,1,0:T(8,128)(2,1)} %bitcast.162), calls=%async_computation.1 | async-start | bytes 12582912 | tf_op jit(solution)/shard_map/all_to_all | solution.py:53
  182.3 8.2 %fusion.13 = f32[2,384,32,24]{1,2,3,0:T(8,128)S(1)} fusion(bf16[32,2,24,2048]{3,2,1,0:T(8,128)(2,1)} %all-to-all-done, bf16[3,2048,2,384]{3,1,2,0:T(8,128)(2,1)} %all-gather.2.cloned.1.call-done), kind=kOutput, calls=%fused_computation.25 | convolution fusion | flops 2415919104 | bytes 11796480 | tf_op jit(solution)/shard_map/sjcd,djf->sjcf/dot_general | solution.py:54
  190.6 9.1 %fusion.37 = (bf16[32,2,24,384]{3,0,2,1:T(8,128)(2,1)S(1)}, f32[2,384,32,24]{1,2,3,0:T(8,128)}) fusion(f32[2,384,32,24]{1,2,3,0:T(8,128)S(1)} %fusion.13, bf16[32,2,24,2048]{3,2,1,0:T(8,128)(2,1)} %all-to-all-done, bf16[3,2048,2,384]{3,1,2,0:T(8,128)(2,1)S(1)} %copy-done.4), kind=kOutput, calls=%fused_computation.46 | convolution fusion | flops 2419458048 | bytes 15335424 | tf_op jit(solution)/shard_map/sjcd,djf->sjcf/dot_general | solution.py:55
  199.7 5.4 convert_bitcast_fusion
  205.1 117.6 %all-to-all-done.1 = bf16[32,2,24,2048]{3,2,1,0:T(8,128)(2,1)} async-done(((bf16[32,2,24,2048]{3,2,1,0:T(8,128)(2,1)}), bf16[32,2,24,2048]{3,2,1,0:T(8,128)(2,1)}, u32[]{:S(2)}, u32[]{:S(2)}) %all-to-all-start.1) | async-done | bytes 6291488 | tf_op jit(solution)/shard_map/all_to_all | solution.py:53
  322.7 8.8 %copy.90 = bf16[32,2,24,2048]{3,2,1,0:T(8,128)(2,1)} copy(bf16[32,2,24,2048]{3,0,2,1:T(8,128)(2,1)} %convert_bitcast_fusion) | data formatting | bytes 12582912 | tf_op jit(solution)/shard_map/optimization_barrier | solution.py:61
  331.4 7.6 %all-to-all-start.2 = ((bf16[32,2,24,2048]{3,2,1,0:T(8,128)(2,1)}), bf16[32,2,24,2048]{3,2,1,0:T(8,128)(2,1)}, u32[]{:S(2)}, u32[]{:S(2)}) async-start(bf16[32,2,24,2048]{3,2,1,0:T(8,128)(2,1)} %copy.90), calls=%async_computation.2 | async-start | bytes 12582912 | tf_op jit(solution)/shard_map/all_to_all | solution.py:62
  339.3 9.5 %fusion.36 = (bf16[32,2,24,384]{3,0,2,1:T(8,128)(2,1)S(1)}, bf16[32,2,24,384]{3,0,2,1:T(8,128)(2,1)S(1)}) fusion(f32[2,384,32,24]{1,2,3,0:T(8,128)} %copy-done.13, f32[2,384,32,24]{1,2,3,0:T(8,128)} %get-tuple-element.60, bf16[32,2,24,2048]{3,2,1,0:T(8,128)(2,1)} %all-to-all-done.1, bf16[3,2048,2,384]{3,1,2,0:T(8,128)(2,1)} %all-gather.2.cloned.1.call-done), kind=kOutput, calls=%fused_computation.44 | convolution fusion | flops 2423586816 | bytes 16515072 | tf_op jit(solution)/shard_map/sjcd,djf->sjcf/dot_general | solution.py:63
  348.8 8.3 %fusion.30 = f32[2,2048,32,24]{1,2,3,0:T(8,128)} fusion(bf16[32,2,24,384]{3,0,2,1:T(8,128)(2,1)S(1)} %get-tuple-element.55, bf16[3,2048,2,384]{3,1,2,0:T(8,128)(2,1)} %all-gather.2.cloned.1.call-done), kind=kOutput, calls=%fused_computation.33 | convolution fusion | flops 2415919104 | bytes 16908288 | tf_op jit(solution)/shard_map/sjcf,djf->sjcd/dot_general | solution.py:73
  357.1 9.4 %fusion = bf16[32,2,24,2048]{3,0,2,1:T(8,128)(2,1)} fusion(f32[2,2048,32,24]{1,2,3,0:T(8,128)} %fusion.30, bf16[32,2,24,384]{3,0,2,1:T(8,128)(2,1)S(1)} %get-tuple-element.54, bf16[3,2048,2,384]{3,1,2,0:T(8,128)(2,1)} %all-gather.2.cloned.1.call-done), kind=kOutput, calls=%fused_computation.5 | convolution fusion | flops 2422210560 | bytes 23199744 | tf_op jit(solution)/shard_map/sjcf,djf->sjcd/dot_general | solution.py:76
  366.5 9.2 %fusion.27 = bf16[2048,1,2,384]{0,3,2,1:T(8,128)(2,1)} fusion(bf16[32,2,24,384]{3,0,2,1:T(8,128)(2,1)S(1)} %get-tuple-element.59, bf16[32,2,24,2048]{3,2,1,0:T(8,128)(2,1)} %all-to-all-done.1), kind=kOutput, calls=%fused_computation.32 | convolution fusion | flops 2417491968 | bytes 10616832 | tf_op jit(solution)/shard_map/sjcd,sjcf->djf/dot_general | solution.py:118
  375.7 9.3 %fusion.24 = bf16[2048,1,2,384]{0,3,2,1:T(8,128)(2,1)} fusion(bf16[32,2,24,384]{3,0,2,1:T(8,128)(2,1)S(1)} %get-tuple-element.54, bf16[32,2,24,2048]{3,2,1,0:T(8,128)(2,1)} %all-to-all-done), kind=kOutput, calls=%fused_computation.31 | convolution fusion | flops 2417491968 | bytes 10616832 | tf_op jit(solution)/shard_map/sjcd,sjcf->djf/dot_general | solution.py:115
  385.0 9.4 %fusion.21 = bf16[2048,1,2,384]{0,3,2,1:T(8,128)(2,1)} fusion(bf16[32,2,24,384]{3,0,2,1:T(8,128)(2,1)S(1)} %get-tuple-element.55, bf16[32,2,24,2048]{3,2,1,0:T(8,128)(2,1)} %all-to-all-done), kind=kOutput, calls=%fused_computation.30 | convolution fusion | flops 2417491968 | bytes 10616832 | tf_op jit(solution)/shard_map/sjcd,sjcf->djf/dot_general | solution.py:112
  394.4 85.6 %all-to-all-done.2 = bf16[32,2,24,2048]{3,2,1,0:T(8,128)(2,1)} async-done(((bf16[32,2,24,2048]{3,2,1,0:T(8,128)(2,1)}), bf16[32,2,24,2048]{3,2,1,0:T(8,128)(2,1)}, u32[]{:S(2)}, u32[]{:S(2)}) %all-to-all-start.2) | async-done | bytes 6291488 | tf_op jit(solution)/shard_map/all_to_all | solution.py:62
  480.0 4.6 convolution_bitcast_fusion
  484.6 7.0 gather_fusion
  493.1 9.1 %pad_maximum_fusion = bf16[2048,3,2,384]{0,3,2,1:T(8,128)(2,1)} fusion(bf16[2048,1,2,384]{0,3,2,1:T(8,128)(2,1)} %fusion.27, bf16[2048,1,2,384]{0,3,2,1:T(8,128)(2,1)} %fusion.24, bf16[2048,1,2,384]{0,3,2,1:T(8,128)(2,1)} %fusion.21), kind=kLoop, calls=%fused_computation.3 | loop fusion | flops 9437184 | bytes 18874368 | tf_op jit(solution)/shard_map/stack | solution.py:122
  502.2 8.9 %copy.91 = bf16[32,2,24,2048]{3,2,1,0:T(8,128)(2,1)} copy(bf16[32,2,24,2048]{3,0,2,1:T(8,128)(2,1)} %fusion) | data formatting | bytes 12582912 | tf_op jit(solution)/shard_map/optimization_barrier | solution.py:79
  511.1 9.1 %all-to-all-start.3 = ((bf16[32,2,24,2048]{3,2,1,0:T(8,128)(2,1)}), bf16[32,2,24,2048]{3,2,1,0:T(8,128)(2,1)}, u32[]{:S(2)}, u32[]{:S(2)}) async-start(bf16[32,2,24,2048]{3,2,1,0:T(8,128)(2,1)} %copy.91), calls=%async_computation.3 | async-start | bytes 12582912 | tf_op jit(solution)/shard_map/all_to_all | solution.py:80
  520.2 40.5 %all-reduce.2.cloned.1.call-done = f32[2048,64]{0,1:T(8,128)} async-done(((f32[2048,64]{0,1:T(8,128)}), f32[2048,64]{0,1:T(8,128)}) %all-reduce.2.cloned.1.call-update) | async-done | bytes 524304 | tf_op jit(solution)/shard_map/psum | solution.py:97
  560.7 100.3 %all-to-all-done.3 = bf16[32,2,24,2048]{3,2,1,0:T(8,128)(2,1)} async-done(((bf16[32,2,24,2048]{3,2,1,0:T(8,128)(2,1)}), bf16[32,2,24,2048]{3,2,1,0:T(8,128)(2,1)}, u32[]{:S(2)}, u32[]{:S(2)}) %all-to-all-start.3) | async-done | bytes 6291488 | tf_op jit(solution)/shard_map/all_to_all | solution.py:80
  664.5 9.5 %all-to-all-start.4 = ((f32[32,1,4096]{2,1,0:T(1,128)}), f32[32,1,4096]{2,1,0:T(1,128)S(1)}, u32[]{:S(2)}, u32[]{:S(2)}) async-start(f32[32,1,4096]{2,1,0:T(1,128)} %reshape.115), calls=%async_computation.5 | async-start | bytes 1048576 | tf_op jit(solution)/shard_map/all_to_all | solution.py:100
  674.1 3.9 fusion.45
  678.0 13.6 %all-to-all-done.4 = f32[32,1,4096]{2,1,0:T(1,128)S(1)} async-done(((f32[32,1,4096]{2,1,0:T(1,128)}), f32[32,1,4096]{2,1,0:T(1,128)S(1)}, u32[]{:S(2)}, u32[]{:S(2)}) %all-to-all-start.4) | async-done | bytes 524320 | tf_op jit(solution)/shard_map/all_to_all | solution.py:100
  696.2 4.9 all-to-all-start.5
  701.0 4.7 fusion.31
  (78 shorter events, 30.4 us)
Async XLA Ops:
  7.2 38.7 %copy-start = (bf16[128,2048]{1,0:T(8,128)(2,1)S(1)}, bf16[128,2048]{1,0:T(8,128)(2,1)}, u32[]{:S(2)}) copy-start(bf16[128,2048]{1,0:T(8,128)(2,1)} %param.13) | copy-start | bytes 1572868
  15.2 30.7 %copy-start.1 = (pred[1536,128]{1,0:T(8,128)(4,1)}, pred[1536,128]{1,0:T(8,128)(4,1)S(1)}, u32[]{:S(2)}) copy-start(pred[1536,128]{1,0:T(8,128)(4,1)S(1)} %fusion.1) | copy-start | bytes 589828
  20.7 11.9 %copy-start.7 = (bf16[256,2,384]{2,1,0:T(2,128)(2,1)S(1)}, bf16[256,2,384]{2,1,0:T(2,128)(2,1)}, u32[]{:S(2)}) copy-start(bf16[256,2,384]{2,1,0:T(2,128)(2,1)} %param.10) | copy-start | bytes 1179652
  20.7 11.9 %copy-start.8 = (bf16[256,2,384]{2,1,0:T(2,128)(2,1)S(1)}, bf16[256,2,384]{2,1,0:T(2,128)(2,1)}, u32[]{:S(2)}) copy-start(bf16[256,2,384]{2,1,0:T(2,128)(2,1)} %param.12) | copy-start | bytes 1179652
  20.7 11.9 %copy-start.9 = (bf16[256,2,384]{2,1,0:T(2,128)(2,1)S(1)}, bf16[256,2,384]{2,1,0:T(2,128)(2,1)}, u32[]{:S(2)}) copy-start(bf16[256,2,384]{2,1,0:T(2,128)(2,1)} %param.11) | copy-start | bytes 1179652
  20.7 13.3 %copy-start.3 = (bf16[128,2048]{1,0:T(8,128)(2,1)S(1)}, bf16[128,2048]{1,0:T(8,128)(2,1)}, u32[]{:S(2)}) copy-start(bf16[128,2048]{1,0:T(8,128)(2,1)} %param.7) | copy-start | bytes 1572868
  20.7 13.3 %copy-start.5 = (bf16[2048,64]{0,1:T(8,128)(2,1)S(1)}, bf16[2048,64]{0,1:T(8,128)(2,1)}, u32[]{:S(2)}) copy-start(bf16[2048,64]{0,1:T(8,128)(2,1)} %param.8) | copy-start | bytes 786436
  20.7 152.4 %all-to-all-start = ((bf16[32,2,24,2048]{3,2,1,0:T(8,128)(2,1)}), bf16[32,2,24,2048]{3,2,1,0:T(8,128)(2,1)}, u32[]{:S(2)}, u32[]{:S(2)}) async-start(bf16[32,2,24,2048]{3,2,1,0:T(8,128)(2,1)} %bitcast.163), calls=%async_computation | async-start | bytes 12582912 | tf_op jit(solution)/shard_map/all_to_all | solution.py:51
  32.3 2.0 copy-start.12
  32.3 150.0 %all-gather.2.cloned.1.call-start = ((), (), s32[]{:S(2)}) async-start(), calls=%async_computation.7 | async-start | bytes 10616832 | tf_op jit(solution)/shard_map/all_gather | solution.py:47
  45.9 127.2 %copy-start.10 = (f32[1536]{0:T(1024)}, f32[1536]{0:T(1024)S(1)}, u32[]{:S(2)}) copy-start(f32[1536]{0:T(1024)S(1)} %select_reduce_fusion) | copy-start | bytes 18436
  173.1 149.5 %all-to-all-start.1 = ((bf16[32,2,24,2048]{3,2,1,0:T(8,128)(2,1)}), bf16[32,2,24,2048]{3,2,1,0:T(8,128)(2,1)}, u32[]{:S(2)}, u32[]{:S(2)}) async-start(bf16[32,2,24,2048]{3,2,1,0:T(8,128)(2,1)} %bitcast.162), calls=%async_computation.1 | async-start | bytes 12582912 | tf_op jit(solution)/shard_map/all_to_all | solution.py:53
  182.3 8.2 %copy-start.4 = (bf16[3,2048,2,384]{3,1,2,0:T(8,128)(2,1)S(1)}, bf16[3,2048,2,384]{3,1,2,0:T(8,128)(2,1)}, u32[]{:S(2)}) copy-start(bf16[3,2048,2,384]{3,1,2,0:T(8,128)(2,1)} %all-gather.2.cloned.1.call-done) | copy-start | bytes 28311556
  190.5 9.1 %copy-start.13 = (f32[2,384,32,24]{1,2,3,0:T(8,128)}, f32[2,384,32,24]{1,2,3,0:T(8,128)S(1)}, u32[]{:S(2)}) copy-start(f32[2,384,32,24]{1,2,3,0:T(8,128)S(1)} %fusion.13) | copy-start | bytes 7077892
  331.4 148.5 %all-to-all-start.2 = ((bf16[32,2,24,2048]{3,2,1,0:T(8,128)(2,1)}), bf16[32,2,24,2048]{3,2,1,0:T(8,128)(2,1)}, u32[]{:S(2)}, u32[]{:S(2)}) async-start(bf16[32,2,24,2048]{3,2,1,0:T(8,128)(2,1)} %copy.90), calls=%async_computation.2 | async-start | bytes 12582912 | tf_op jit(solution)/shard_map/all_to_all | solution.py:62
  339.0 221.7 %all-reduce.2.cloned.1.call-start = ((), (), s32[]{:S(2)}) async-start(), calls=%async_computation.8 | async-start | bytes 1048576 | tf_op jit(solution)/shard_map/psum | solution.py:97
  493.0 212.7 %reduce-scatter.2.cloned.1.call-start = ((), (), s32[]{:S(2)}) async-start(), calls=%async_computation.9 | async-start | bytes 10616832 | tf_op jit(solution)/shard_map/reduce_scatter | solution.py:121
  511.1 150.0 %all-to-all-start.3 = ((bf16[32,2,24,2048]{3,2,1,0:T(8,128)(2,1)}), bf16[32,2,24,2048]{3,2,1,0:T(8,128)(2,1)}, u32[]{:S(2)}, u32[]{:S(2)}) async-start(bf16[32,2,24,2048]{3,2,1,0:T(8,128)(2,1)} %copy.91), calls=%async_computation.3 | async-start | bytes 12582912 | tf_op jit(solution)/shard_map/all_to_all | solution.py:80
  520.2 153.9 %copy-start.2 = (pred[1536,128]{1,0:T(8,128)(4,1)S(1)}, pred[1536,128]{1,0:T(8,128)(4,1)}, u32[]{:S(2)}) copy-start(pred[1536,128]{1,0:T(8,128)(4,1)} %copy-done.1) | copy-start | bytes 589828
  520.2 153.9 %copy-start.11 = (f32[1536]{0:T(1024)S(1)}, f32[1536]{0:T(1024)}, u32[]{:S(2)}) copy-start(f32[1536]{0:T(1024)} %copy-done.10) | copy-start | bytes 18436
  664.5 27.1 %all-to-all-start.4 = ((f32[32,1,4096]{2,1,0:T(1,128)}), f32[32,1,4096]{2,1,0:T(1,128)S(1)}, u32[]{:S(2)}, u32[]{:S(2)}) async-start(f32[32,1,4096]{2,1,0:T(1,128)} %reshape.115), calls=%async_computation.5 | async-start | bytes 1048576 | tf_op jit(solution)/shard_map/all_to_all | solution.py:100
  696.2 21.8 %all-to-all-start.5 = ((f32[32,1,4096]{2,1,0:T(1,128)}), f32[32,1,4096]{2,1,0:T(1,128)S(1)}, u32[]{:S(2)}, u32[]{:S(2)}) async-start(f32[32,1,4096]{2,1,0:T(1,128)} %reshape.117), calls=%async_computation.6 | async-start | bytes 1048576 | tf_op jit(solution)/shard_map/all_to_all | solution.py:103
  705.7 8.5 %copy-start.6 = (bf16[2048,64]{0,1:T(8,128)(2,1)S(1)}, bf16[2048,64]{0,1:T(8,128)(2,1)}, u32[]{:S(2)}) copy-start(bf16[2048,64]{0,1:T(8,128)(2,1)} %param.8) | copy-start | bytes 786436
Sparse Core Ops, SparseCore 0:
  35.0 57.6 all-gather.1
  493.1 67.5 all-reduce.1
  563.3 59.0 reduce-scatter.1

commit v7 on v3

--- a/solution.py
+++ b/solution.py
@@ -95,12 +95,15 @@
     choice_slope = gate_weights * centred
     logit_slope = jnp.sum(onehot * choice_slope[:, :, None], axis=1)
     router_local = jnp.dot(tokens.astype(jnp.float32).T, logit_slope, precision=highest)
-    row_parts = router_local.reshape(owners, model_width // owners, experts_total)
-    row_parts = lax.all_to_all(row_parts, "expert", split_axis=0, concat_axis=0, tiled=True)
-    row_block = lax.psum(jnp.sum(row_parts, axis=0), "dp")
-    row_copies = jnp.broadcast_to(row_block[None], (owners,) + row_block.shape)
+    devices_all = owners * lax.axis_size("dp")
+    row_parts = router_local.reshape(devices_all, model_width // devices_all, experts_total)
+    row_parts = lax.all_to_all(
+        row_parts, ("dp", "expert"), split_axis=0, concat_axis=0, tiled=True
+    )
+    row_block = jnp.sum(row_parts, axis=0)
+    row_copies = jnp.broadcast_to(row_block[None], (devices_all,) + row_block.shape)
     router_grad = lax.all_to_all(
-        row_copies, "expert", split_axis=0, concat_axis=0, tiled=True
+        row_copies, ("dp", "expert"), split_axis=0, concat_axis=0, tiled=True
     ).reshape(model_width, experts_total)
     back_rows = slopes_back.reshape(slot_count, model_width)
     input_sum = lax.dot_general(

time: 731 us -> 722 us (0.988)
  blocking collectives: 50.2 us -> 32.6 us
  waiting for transfers between devices: 454 us -> 465 us
    psum x1 -> x0, blocking collectives: 23.6 us -> none  [shards(): row_block = lax.psum(jnp.sum(row_parts, axis=0), 'dp')]
where the time goes in v7:
time: 722 us; the launch traced here: 712 us
  waiting for transfers between devices  465 us (64%)
  matrix products  97.4 us (13%)
  starting transfers between devices  41.4 us (6%)
  local copies, waits for them, and re-layouts  34.8 us (5%)
  blocking collectives  32.6 us (5%)
  other arithmetic  26.3 us (4%)
  between operations  14.5 us (2%)
    all_to_all x1, waiting for transfers between devices, shards(): lax.all_to_all(pick_slope, 'expert', split_axis=0, concat_axis=0, tiled=T...  123 us
    all_to_all x1, waiting for transfers between devices, shards(): lax.all_to_all(send_tokens, 'expert', split_axis=0, concat_axis=0, tiled=...  122 us
    all_to_all x1, waiting for transfers between devices, shards(): lax.all_to_all(outputs, 'expert', split_axis=0, concat_axis=0, tiled=True)  93.5 us
    all_to_all x1, waiting for transfers between devices, shards(): lax.all_to_all(send_slopes, 'expert', split_axis=0, concat_axis=0, tiled=...  65.9 us
    all_to_all x1, blocking collectives, shards(): lax.all_to_all(row_parts, ('dp', 'expert'), split_axis=0, concat_axis=0,...  32.6 us
    all_gather x1, waiting for transfers between devices, shards(): lax.all_gather(up_matrix, 'dp', axis=0, tiled=True)  23.9 us
    all_gather x1, waiting for transfers between devices, shards(): lax.all_gather(down_matrix, 'dp', axis=0, tiled=True)  23.3 us
  transfers between devices with their start and end apart: 9, of which 7 were waited for; matrix products, arithmetic and copies ran while one was open for 18% of the time, Pallas kernels for 0%

profile of v7, /device:TPU:32, one launch (start us, length us, event | category | flops | bytes accessed | tf_op | source)
XLA Modules:
  0.0 712.4 jit_solution(18420093428475480773)
XLA Ops:
  9.6 5.6 fusion.1
  15.2 5.5 convolution_convert_fusion
  20.7 11.5 %all-to-all-start = ((bf16[32,2,24,2048]{3,2,1,0:T(8,128)(2,1)}), bf16[32,2,24,2048]{3,2,1,0:T(8,128)(2,1)}, u32[]{:S(2)}, u32[]{:S(2)}) async-start(bf16[32,2,24,2048]{3,2,1,0:T(8,128)(2,1)} %bitcast.146), calls=%async_computation | async-start | bytes 12582912 | tf_op jit(solution)/shard_map/all_to_all | solution.py:52
  34.9 11.5 %select_reduce_fusion = f32[1536]{0:T(1024)S(1)} fusion(f32[128,8]{0,1:T(8,128)S(1)} %exponential_divide_fusion, s32[128,8]{0,1:T(8,128)S(1)} %get-tuple-element.43), kind=kLoop, calls=%fused_computation.10 | loop fusion | flops 4717056 | bytes 14336 | tf_op jit(solution)/shard_map/reduce_sum | solution.py:35
  47.0 4.4 multiply_convert_fusion
  51.4 121.7 %all-to-all-done = bf16[32,2,24,2048]{3,2,1,0:T(8,128)(2,1)} async-done(((bf16[32,2,24,2048]{3,2,1,0:T(8,128)(2,1)}), bf16[32,2,24,2048]{3,2,1,0:T(8,128)(2,1)}, u32[]{:S(2)}, u32[]{:S(2)}) %all-to-all-start) | async-done | bytes 6291488 | tf_op jit(solution)/shard_map/all_to_all | solution.py:52
  173.1 8.6 %all-to-all-start.1 = ((bf16[32,2,24,2048]{3,2,1,0:T(8,128)(2,1)}), bf16[32,2,24,2048]{3,2,1,0:T(8,128)(2,1)}, u32[]{:S(2)}, u32[]{:S(2)}) async-start(bf16[32,2,24,2048]{3,2,1,0:T(8,128)(2,1)} %bitcast.145), calls=%async_computation.1 | async-start | bytes 12582912 | tf_op jit(solution)/shard_map/all_to_all | solution.py:54
  184.0 8.6 %fusion.13 = f32[2,32,24,384]{3,2,1,0:T(8,128)} fusion(bf16[32,2,24,2048]{3,2,1,0:T(8,128)(2,1)} %all-to-all-done, bf16[2048,2,384]{2,0,1:T(8,128)(2,1)} %all-gather.4.cloned.1.call-done), kind=kOutput, calls=%fused_computation.25 | convolution fusion | flops 2415919104 | bytes 11796480 | tf_op jit(solution)/shard_map/sjcd,djf->sjcf/dot_general | solution.py:55
  192.6 23.9 %all-gather.6.cloned.1.call-done = bf16[2048,2,384]{2,0,1:T(8,128)(2,1)} async-done(((bf16[256,2,384]{2,0,1:T(8,128)(2,1)}), bf16[2048,2,384]{2,0,1:T(8,128)(2,1)}) %all-gather.6.cloned.1.call-update) | async-done | bytes 3145744 | tf_op jit(solution)/shard_map/all_gather | solution.py:49
  216.5 9.4 %fusion.43 = (bf16[32,2,24,384]{3,2,0,1:T(8,128)(2,1)S(1)}, f32[2,32,24,384]{3,2,1,0:T(8,128)}) fusion(f32[2,32,24,384]{3,2,1,0:T(8,128)} %fusion.13, bf16[2048,2,384]{2,0,1:T(8,128)(2,1)} %all-gather.6.cloned.1.call-done, bf16[32,2,24,2048]{3,2,1,0:T(8,128)(2,1)} %all-to-all-done), kind=kOutput, calls=%fused_computation.49 | convolution fusion | flops 2419458048 | bytes 15335424 | tf_op jit(solution)/shard_map/sjcd,djf->sjcf/dot_general | solution.py:56
  225.9 23.3 %all-gather.8.cloned.1.call-done = bf16[2048,2,384]{2,0,1:T(8,128)(2,1)} async-done(((bf16[256,2,384]{2,0,1:T(8,128)(2,1)}), bf16[2048,2,384]{2,0,1:T(8,128)(2,1)}) %all-gather.8.cloned.1.call-update) | async-done | bytes 3145744 | tf_op jit(solution)/shard_map/all_gather | solution.py:50
  249.1 7.2 %convert_bitcast_fusion = bf16[32,2,24,2048]{3,2,0,1:T(8,128)(2,1)} fusion(bf16[32,2,24,384]{3,2,0,1:T(8,128)(2,1)S(1)} %get-tuple-element.49, bf16[2048,2,384]{2,0,1:T(8,128)(2,1)} %all-gather.8.cloned.1.call-done), kind=kOutput, calls=%fused_computation.9 | convolution fusion | flops 2419064832 | bytes 10616832 | tf_op jit(solution)/shard_map/sjcf,djf->sjcd/dot_general | solution.py:58
  256.4 65.9 %all-to-all-done.1 = bf16[32,2,24,2048]{3,2,1,0:T(8,128)(2,1)} async-done(((bf16[32,2,24,2048]{3,2,1,0:T(8,128)(2,1)}), bf16[32,2,24,2048]{3,2,1,0:T(8,128)(2,1)}, u32[]{:S(2)}, u32[]{:S(2)}) %all-to-all-start.1) | async-done | bytes 6291488 | tf_op jit(solution)/shard_map/all_to_all | solution.py:54
  322.2 6.6 copy.90
  328.8 7.5 %all-to-all-start.2 = ((bf16[32,2,24,2048]{3,2,1,0:T(8,128)(2,1)}), bf16[32,2,24,2048]{3,2,1,0:T(8,128)(2,1)}, u32[]{:S(2)}, u32[]{:S(2)}) async-start(bf16[32,2,24,2048]{3,2,1,0:T(8,128)(2,1)} %copy.90), calls=%async_computation.2 | async-start | bytes 12582912 | tf_op jit(solution)/shard_map/all_to_all | solution.py:63
  336.6 9.2 %fusion.42 = (bf16[32,2,24,384]{3,2,0,1:T(8,128)(2,1)S(1)}, bf16[32,2,24,384]{3,2,0,1:T(8,128)(2,1)S(1)}) fusion(f32[2,32,24,384]{3,2,1,0:T(8,128)} %fusion.13, f32[2,32,24,384]{3,2,1,0:T(8,128)} %get-tuple-element.50, bf16[2048,2,384]{2,0,1:T(8,128)(2,1)} %all-gather.8.cloned.1.call-done, bf16[32,2,24,2048]{3,2,1,0:T(8,128)(2,1)} %all-to-all-done.1), kind=kOutput, calls=%fused_computation.47 | convolution fusion | flops 2423586816 | bytes 16515072 | tf_op jit(solution)/shard_map/sjcd,djf->sjcf/dot_general | solution.py:64
  345.8 5.5 fusion.34
  351.3 5.5 fusion.31
  356.7 5.5 fusion.28
  362.2 4.4 pad_maximum_fusion
  366.8 8.5 %fusion.23 = f32[2,32,24,2048]{3,2,1,0:T(8,128)} fusion(bf16[32,2,24,384]{3,2,0,1:T(8,128)(2,1)S(1)} %get-tuple-element.45, bf16[2048,2,384]{2,0,1:T(8,128)(2,1)} %all-gather.4.cloned.1.call-done), kind=kOutput, calls=%fused_computation.29 | convolution fusion | flops 2415919104 | bytes 16908288 | tf_op jit(solution)/shard_map/sjcf,djf->sjcd/dot_general | solution.py:74
  375.3 8.4 %fusion = bf16[32,2,24,2048]{3,2,0,1:T(8,128)(2,1)} fusion(f32[2,32,24,2048]{3,2,1,0:T(8,128)} %fusion.23, bf16[32,2,24,384]{3,2,0,1:T(8,128)(2,1)S(1)} %get-tuple-element.44, bf16[2048,2,384]{2,0,1:T(8,128)(2,1)S(1)} %copy-done.5), kind=kOutput, calls=%fused_computation.5 | convolution fusion | flops 2422210560 | bytes 23199744 | tf_op jit(solution)/shard_map/sjcf,djf->sjcd/dot_general | solution.py:77
  383.8 93.5 %all-to-all-done.2 = bf16[32,2,24,2048]{3,2,1,0:T(8,128)(2,1)} async-done(((bf16[32,2,24,2048]{3,2,1,0:T(8,128)(2,1)}), bf16[32,2,24,2048]{3,2,1,0:T(8,128)(2,1)}, u32[]{:S(2)}, u32[]{:S(2)}) %all-to-all-start.2) | async-done | bytes 6291488 | tf_op jit(solution)/shard_map/all_to_all | solution.py:63
  477.2 4.6 convolution_bitcast_fusion
  481.9 7.0 gather_fusion
  490.6 32.6 %all_to_all.30 = f32[256,1,512]{2,1,0:T(1,128)S(1)} all-to-all(f32[256,1,512]{2,1,0:T(1,128)S(1)} %reshape.115), channel_id=1, replica_groups=mesh['dp'=8,'expert'=32] {'dp','expert'}, dimensions={0} | all-to-all | bytes 1048576 | tf_op jit(solution)/shard_map/all_to_all | solution.py:100
  527.6 6.9 all-to-all-start.5
  534.5 6.6 copy.91
  541.1 13.7 %all-to-all-done.5 = f32[256,1,512]{2,1,0:T(1,128)S(1)} async-done(((f32[256,1,512]{2,1,0:T(1,128)}), f32[256,1,512]{2,1,0:T(1,128)S(1)}, u32[]{:S(2)}, u32[]{:S(2)}) %all-to-all-start.5) | async-done | bytes 524320 | tf_op jit(solution)/shard_map/all_to_all | solution.py:105
  554.8 5.7 all-to-all-start.3
  564.4 4.7 fusion.37
  576.9 123.3 %all-to-all-done.3 = bf16[32,2,24,2048]{3,2,1,0:T(8,128)(2,1)} async-done(((bf16[32,2,24,2048]{3,2,1,0:T(8,128)(2,1)}), bf16[32,2,24,2048]{3,2,1,0:T(8,128)(2,1)}, u32[]{:S(2)}, u32[]{:S(2)}) %all-to-all-start.3) | async-done | bytes 6291488 | tf_op jit(solution)/shard_map/all_to_all | solution.py:81
  (96 shorter events, 31.3 us)
Async XLA Ops:
  7.2 39.9 %copy-start = (bf16[128,2048]{1,0:T(8,128)(2,1)S(1)}, bf16[128,2048]{1,0:T(8,128)(2,1)}, u32[]{:S(2)}) copy-start(bf16[128,2048]{1,0:T(8,128)(2,1)} %param.13) | copy-start | bytes 1572868
  9.6 25.4 %copy-start.17 = (s32[128,8]{0,1:T(8,128)}, s32[128,8]{0,1:T(8,128)S(1)}, u32[]{:S(2)}) copy-start(s32[128,8]{0,1:T(8,128)S(1)} %get-tuple-element.43) | copy-start | bytes 12292
  15.2 31.2 %copy-start.1 = (pred[1536,128]{1,0:T(8,128)(4,1)}, pred[1536,128]{1,0:T(8,128)(4,1)S(1)}, u32[]{:S(2)}) copy-start(pred[1536,128]{1,0:T(8,128)(4,1)S(1)} %fusion.1) | copy-start | bytes 589828
  20.7 11.9 %copy-start.8 = (bf16[256,2,384]{2,1,0:T(2,128)(2,1)S(1)}, bf16[256,2,384]{2,1,0:T(2,128)(2,1)}, u32[]{:S(2)}) copy-start(bf16[256,2,384]{2,1,0:T(2,128)(2,1)} %param.10) | copy-start | bytes 1179652
  20.7 12.7 %copy-start.3 = (bf16[128,2048]{1,0:T(8,128)(2,1)S(1)}, bf16[128,2048]{1,0:T(8,128)(2,1)}, u32[]{:S(2)}) copy-start(bf16[128,2048]{1,0:T(8,128)(2,1)} %param.7) | copy-start | bytes 1572868
  20.7 12.7 %copy-start.6 = (bf16[2048,64]{0,1:T(8,128)(2,1)S(1)}, bf16[2048,64]{0,1:T(8,128)(2,1)}, u32[]{:S(2)}) copy-start(bf16[2048,64]{0,1:T(8,128)(2,1)} %param.8) | copy-start | bytes 786436
  20.7 13.1 %copy-start.15 = (s32[128,8]{0,1:T(8,128)S(1)}, s32[128,8]{0,1:T(8,128)}, u32[]{:S(2)}) copy-start(s32[128,8]{0,1:T(8,128)} %param.9) | copy-start | bytes 12292
  20.7 152.3 %all-to-all-start = ((bf16[32,2,24,2048]{3,2,1,0:T(8,128)(2,1)}), bf16[32,2,24,2048]{3,2,1,0:T(8,128)(2,1)}, u32[]{:S(2)}, u32[]{:S(2)}) async-start(bf16[32,2,24,2048]{3,2,1,0:T(8,128)(2,1)} %bitcast.146), calls=%async_computation | async-start | bytes 12582912 | tf_op jit(solution)/shard_map/all_to_all | solution.py:52
  32.3 151.7 %all-gather.4.cloned.1.call-start = ((), (), s32[]{:S(2)}) async-start(), calls=%async_computation.7 | async-start | bytes 3538944 | tf_op jit(solution)/shard_map/all_gather | solution.py:48
  33.8 0.6 copy-start.13
  34.4 0.5 copy-start.19
  46.4 0.6 copy-start.11
  173.1 8.7 %copy-start.9 = (bf16[256,2,384]{2,1,0:T(2,128)(2,1)S(1)}, bf16[256,2,384]{2,1,0:T(2,128)(2,1)}, u32[]{:S(2)}) copy-start(bf16[256,2,384]{2,1,0:T(2,128)(2,1)} %param.11) | copy-start | bytes 1179652
  173.1 10.1 %copy-start.10 = (bf16[256,2,384]{2,1,0:T(2,128)(2,1)S(1)}, bf16[256,2,384]{2,1,0:T(2,128)(2,1)}, u32[]{:S(2)}) copy-start(bf16[256,2,384]{2,1,0:T(2,128)(2,1)} %param.12) | copy-start | bytes 1179652
  173.1 149.2 %all-to-all-start.1 = ((bf16[32,2,24,2048]{3,2,1,0:T(8,128)(2,1)}), bf16[32,2,24,2048]{3,2,1,0:T(8,128)(2,1)}, u32[]{:S(2)}, u32[]{:S(2)}) async-start(bf16[32,2,24,2048]{3,2,1,0:T(8,128)(2,1)} %bitcast.145), calls=%async_computation.1 | async-start | bytes 12582912 | tf_op jit(solution)/shard_map/all_to_all | solution.py:54
  181.7 34.8 %all-gather.6.cloned.1.call-start = ((), (), s32[]{:S(2)}) async-start(), calls=%async_computation.8 | async-start | bytes 3538944 | tf_op jit(solution)/shard_map/all_gather | solution.py:49
  182.6 66.6 %all-gather.8.cloned.1.call-start = ((), (), s32[]{:S(2)}) async-start(), calls=%async_computation.9 | async-start | bytes 3538944 | tf_op jit(solution)/shard_map/all_gather | solution.py:50
  225.9 30.5 %copy-start.21 = (bf16[32,2,24,384]{3,2,0,1:T(8,128)(2,1)}, bf16[32,2,24,384]{3,2,0,1:T(8,128)(2,1)S(1)}, u32[]{:S(2)}) copy-start(bf16[32,2,24,384]{3,2,0,1:T(8,128)(2,1)S(1)} %get-tuple-element.49) | copy-start | bytes 3538948
  328.8 148.4 %all-to-all-start.2 = ((bf16[32,2,24,2048]{3,2,1,0:T(8,128)(2,1)}), bf16[32,2,24,2048]{3,2,1,0:T(8,128)(2,1)}, u32[]{:S(2)}, u32[]{:S(2)}) async-start(bf16[32,2,24,2048]{3,2,1,0:T(8,128)(2,1)} %copy.90), calls=%async_computation.2 | async-start | bytes 12582912 | tf_op jit(solution)/shard_map/all_to_all | solution.py:63
  336.3 236.0 %reduce-scatter.2.cloned.1.call-start = ((), (), s32[]{:S(2)}) async-start(), calls=%async_computation.10 | async-start | bytes 10616832 | tf_op jit(solution)/shard_map/reduce_scatter | solution.py:123
  336.5 9.2 %copy-start.22 = (bf16[32,2,24,384]{3,2,0,1:T(8,128)(2,1)S(1)}, bf16[32,2,24,384]{3,2,0,1:T(8,128)(2,1)}, u32[]{:S(2)}) copy-start(bf16[32,2,24,384]{3,2,0,1:T(8,128)(2,1)} %copy-done.21) | copy-start | bytes 3538948
  366.8 8.5 %copy-start.5 = (bf16[2048,2,384]{2,0,1:T(8,128)(2,1)S(1)}, bf16[2048,2,384]{2,0,1:T(8,128)(2,1)}, u32[]{:S(2)}) copy-start(bf16[2048,2,384]{2,0,1:T(8,128)(2,1)} %all-gather.6.cloned.1.call-done) | copy-start | bytes 9437188
  481.9 7.2 %copy-start.14 = (f32[128,8]{0,1:T(8,128)S(1)}, f32[128,8]{0,1:T(8,128)}, u32[]{:S(2)}) copy-start(f32[128,8]{0,1:T(8,128)} %copy-done.13) | copy-start | bytes 12292
  481.9 7.2 %copy-start.18 = (s32[128,8]{0,1:T(8,128)S(1)}, s32[128,8]{0,1:T(8,128)}, u32[]{:S(2)}) copy-start(s32[128,8]{0,1:T(8,128)} %copy-done.17) | copy-start | bytes 12292
  481.9 7.2 %copy-start.20 = (f32[128]{0:T(128)S(1)}, f32[128]{0:T(128)}, u32[]{:S(2)}) copy-start(f32[128]{0:T(128)} %copy-done.19) | copy-start | bytes 1540
  481.9 7.3 %copy-start.16 = (s32[128,8]{0,1:T(8,128)S(1)}, s32[128,8]{0,1:T(8,128)}, u32[]{:S(2)}) copy-start(s32[128,8]{0,1:T(8,128)} %param.9) | copy-start | bytes 12292
  481.9 7.3 %copy-start.4 = (bf16[128,2048]{1,0:T(8,128)(2,1)S(1)}, bf16[128,2048]{1,0:T(8,128)(2,1)}, u32[]{:S(2)}) copy-start(bf16[128,2048]{1,0:T(8,128)(2,1)} %param.7) | copy-start | bytes 1572868
  527.6 27.2 %all-to-all-start.5 = ((f32[256,1,512]{2,1,0:T(1,128)}), f32[256,1,512]{2,1,0:T(1,128)S(1)}, u32[]{:S(2)}, u32[]{:S(2)}) async-start(f32[256,1,512]{2,1,0:T(1,128)} %reshape.117), calls=%async_computation.6 | async-start | bytes 1048576 | tf_op jit(solution)/shard_map/all_to_all | solution.py:105
  541.0 19.4 %copy-start.2 = (pred[1536,128]{1,0:T(8,128)(4,1)S(1)}, pred[1536,128]{1,0:T(8,128)(4,1)}, u32[]{:S(2)}) copy-start(pred[1536,128]{1,0:T(8,128)(4,1)} %copy-done.1) | copy-start | bytes 589828
  541.1 19.4 %copy-start.12 = (f32[1536]{0:T(1024)S(1)}, f32[1536]{0:T(1024)}, u32[]{:S(2)}) copy-start(f32[1536]{0:T(1024)} %copy-done.11) | copy-start | bytes 18436
  554.8 145.5 %all-to-all-start.3 = ((bf16[32,2,24,2048]{3,2,1,0:T(8,128)(2,1)}), bf16[32,2,24,2048]{3,2,1,0:T(8,128)(2,1)}, u32[]{:S(2)}, u32[]{:S(2)}) async-start(bf16[32,2,24,2048]{3,2,1,0:T(8,128)(2,1)} %copy.91), calls=%async_computation.3 | async-start | bytes 12582912 | tf_op jit(solution)/shard_map/all_to_all | solution.py:81
  700.2 3.9 copy-start.7
Sparse Core Ops, SparseCore 0:
  35.5 31.2 all-gather.3
  184.9 31.5 all-gather.5
  218.9 30.1 all-gather.7
  366.8 61.3 reduce-scatter.1
